TPU v7x, 1024 devices: a whole 8x8x8 slice. The times are simulated.
1024 devices in a mesh: grp: 32 (over y, x_lo), slab: 32 (over z, x_hi, core).
Axes of the slice: x: 8 (x_hi: 2, x_lo: 4; x = x_hi * 4 + x_lo), y: 8, z: 8, core: 2. Of those that a mesh axis runs over, the one named last changes fastest.
Arguments:
- tiles: bfloat16 [32768, 2, 8, 512], P(('grp', 'slab')), may hold values from -6 to 6
- conv_weight: bfloat16 [576, 64], replicated, may hold values from -0.25 to 0.25
- assignment: int32 [32768, 1], P(('grp', 'slab')), may hold values from 0 to 31; in each aligned block of 32 rows (0 to 31, 32 to 63, ...) at most 2 rows name the same one
- occupancy: int32 [32768], P(('grp', 'slab')), may hold values 0 or 1
- cotangent: bfloat16 [65536, 2, 8, 512], P(('grp', 'slab')), may hold values from -6 to 6
Outputs:
- activations: bfloat16 [65536, 2, 8, 512], P(('grp', 'slab'))
- input_grad: bfloat16 [32768, 2, 8, 512], P(('grp', 'slab'))
- weight_grad: float32 [576, 64], replicated
Inputs may be any that keep to these rules, and one draw needn't show every extreme that they name: `assignment`: the trainer of a tile, an index along slab within the owner's group; among the 32 tiles of one owner at most 2 have the same trainer. `occupancy`: only tiles with 1 are trained.
All inputs are finite; a program needn't handle non-finite values. No bound on the sum of `occupancy` on one device may be relied on, other than what follows from the above.
Results may differ from a plain program's by a relative error of at most 0.0049.
Values may be sent and summed in bfloat16 or wider, within the bound.
No kernel may reach another device: no remote copies, remote signals or barrier semaphores. Data moves between devices by JAX's collectives and lax.ppermute only.
A program may use at most 32 MiB of HBM per device.

v0:
```python
import math

import jax
import jax.numpy as jnp
from jax import lax
from jax.sharding import PartitionSpec as P

C = 64
TD = 2
TH = 8
TW = 8


def cut_along(x, dim, size):
    before, after = (x.shape[:dim], x.shape[dim + 1 :])
    return jnp.moveaxis(x.reshape(*before, size, -1, *after), dim, 0)


def sent_and_summed(x, axis, dim):
    size = lax.axis_size(axis)
    pieces = lax.all_to_all(cut_along(x, dim, size), axis, 0, 0, tiled=True)
    return jnp.sum(pieces, axis=0)


def sent_to_all(x, axis):
    size = lax.axis_size(axis)
    return lax.all_to_all(jnp.broadcast_to(x[None], (size, *x.shape)), axis, 0, 0, tiled=True)


def over_copies(x, axis):
    everything = sent_to_all(x, axis)
    return jnp.sum(everything, axis=0)


def joined_along(pieces, dim):
    pieces = jnp.moveaxis(pieces, 0, dim)
    dims = pieces.shape
    return pieces.reshape(*dims[:dim], dims[dim] * dims[dim + 1], *dims[dim + 2 :])


def gathered_copies(x, axis, dim):
    return joined_along(sent_to_all(x, axis), dim)


def conv_forward(planes, kernel):
    return lax.conv_general_dilated(
        planes,
        kernel,
        (1, 1),
        ((1, 1), (1, 1)),
        dimension_numbers=("NHWC", "HWIO", "NHWC"),
        preferred_element_type=jnp.float32,
    )


def conv_input_grad(grad_planes, kernel):
    flipped = jnp.transpose(kernel[::-1, ::-1, :, :], (0, 1, 3, 2))
    return lax.conv_general_dilated(
        grad_planes,
        flipped,
        (1, 1),
        ((1, 1), (1, 1)),
        dimension_numbers=("NHWC", "HWIO", "NHWC"),
        preferred_element_type=jnp.float32,
    )


def conv_kernel_grad(planes, grad_planes):
    return lax.conv_general_dilated(
        planes,
        grad_planes,
        (1, 1),
        ((1, 1), (1, 1)),
        dimension_numbers=("CHWN", "IHWO", "HWNC"),
        preferred_element_type=jnp.float32,
    )


def layer_local(tile_set, kernel, upstream, mask):
    count = tile_set.shape[0]
    planes = tile_set.reshape(count * TD, TH, TW, C)
    pre = conv_forward(planes, kernel)
    sig = jax.nn.sigmoid(pre)
    act = (pre * sig).astype(jnp.bfloat16).reshape(count, TD, TH, TW * C)
    slope = sig * (1.0 + pre * (1.0 - sig))
    grad_pre = upstream.reshape(count * TD, TH, TW, C).astype(jnp.float32) * slope
    plane_mask = jnp.repeat(mask, TD)
    grad_pre = grad_pre * plane_mask[:, None, None, None]
    grad_pre = grad_pre.astype(jnp.bfloat16)
    back = conv_input_grad(grad_pre, kernel)
    wgrad = conv_kernel_grad(planes, grad_pre).reshape(9 * C, C)
    back = back * plane_mask[:, None, None, None]
    return (act, back.astype(jnp.bfloat16).reshape(count, TD, TH, TW * C), wgrad)


def local(tiles, conv_weight, assignment, occupancy, cotangent):
    n_slab = lax.axis_size("slab")
    n_group = lax.axis_size("grp")
    per_owner = tiles.shape[0]
    capacity = max(2, -(-per_owner // n_slab))
    slot_count = n_slab * capacity
    targets = assignment[:, 0]
    same = targets[:, None] == targets[None, :]
    before = jnp.arange(per_owner)[None, :] < jnp.arange(per_owner)[:, None]
    ranks = jnp.sum((same & before).astype(jnp.int32), axis=1)
    slot_ids = targets * capacity + ranks
    placer = (
        (jnp.arange(slot_count)[:, None] == slot_ids[None, :]) & (occupancy[None, :] == 1)
    ).astype(jnp.bfloat16)
    kernel = conv_weight.reshape(3, 3, C, C)
    upstream_slots = lax.all_to_all(cotangent, "slab", split_axis=0, concat_axis=0, tiled=True)
    upstream = jnp.einsum(
        "sk,sdhx->kdhx", placer, upstream_slots, preferred_element_type=jnp.float32
    ).astype(jnp.bfloat16)
    mask = occupancy.astype(jnp.float32)
    act_tiles, input_grad, wgrad = layer_local(tiles, kernel, upstream, mask)
    outgoing = jnp.einsum(
        "sk,kdhx->sdhx", placer, act_tiles, preferred_element_type=jnp.float32
    ).astype(jnp.bfloat16)
    activations = lax.all_to_all(outgoing, "slab", split_axis=0, concat_axis=0, tiled=True)
    share = sent_and_summed(wgrad.reshape(-1), "slab", 0)
    share = over_copies(share, "grp")
    summed = gathered_copies(share, "slab", 0).reshape(9 * C, C)
    scale = 1.0 / math.sqrt(per_owner * n_group * n_slab * TD * TH * TW)
    return (activations, input_grad, summed * scale)


def solution(mesh):
    in_specs = (
        P(("grp", "slab"), None, None, None),
        P(),
        P(("grp", "slab"), None),
        P(("grp", "slab")),
        P(("grp", "slab"), None, None, None),
    )
    out_specs = (P(("grp", "slab"), None, None, None), P(("grp", "slab"), None, None, None), P())
    return jax.shard_map(local, mesh=mesh, in_specs=in_specs, out_specs=out_specs, check_vma=False)
```

profile of v0, /device:TPU:1, one launch (start us, length us, event | category | flops | bytes accessed | tf_op | source)
XLA Modules:
  0.0 158.8 jit_solution(3971672178583337344)
XLA Ops:
  0.6 0.0 copy-start.3
  0.6 0.0 copy-start.2
  0.7 0.0 copy-start.1
  0.7 23.4 %all-to-all-start.1 = ((bf16[64,2,8,512]{3,2,1,0:T(8,128)(2,1)}), bf16[64,2,8,512]{3,2,1,0:T(8,128)(2,1)S(1)}, u32[]{:S(2)}, u32[]{:S(2)}) async-start(bf16[64,2,8,512]{3,2,1,0:T(8,128)(2,1)} %param.9), calls=%async_computation.1 | async-start | bytes 2097152 | tf_op jit(solution)/shard_map/all_to_all | solution.py:111
  24.1 0.0 copy-done.3
  24.1 0.0 copy-start.4
  24.1 0.1 broadcast_in_dim.6
  24.2 0.1 mul.53
  24.3 0.0 copy-done.2
  24.3 0.1 copy.49
  24.4 0.0 copy-done.1
  24.4 0.5 reshape.51
  25.0 2.0 %copy.58 = bf16[64,8,8,64]{0,3,2,1:T(8,128)(2,1)} copy(bf16[64,8,8,64]{3,2,1,0:T(8,128)(2,1)S(1)} %reshape.51) | data formatting | bytes 1048576 | tf_op jit(solution)/shard_map/reshape | solution.py:81
  27.0 0.0 copy-done.4
  27.0 0.2 convert_reduce_fusion
  27.2 26.9 %all-to-all-done.1 = bf16[64,2,8,512]{3,2,1,0:T(8,128)(2,1)S(1)} async-done(((bf16[64,2,8,512]{3,2,1,0:T(8,128)(2,1)}), bf16[64,2,8,512]{3,2,1,0:T(8,128)(2,1)S(1)}, u32[]{:S(2)}, u32[]{:S(2)}) %all-to-all-start.1) | async-done | bytes 1048608 | tf_op jit(solution)/shard_map/all_to_all | solution.py:111
  54.0 1.3 fusion.2
  55.3 0.6 copy.55
  56.0 0.4 reshape.55
  56.4 0.0 copy-start
  56.4 5.4 %fusion.1 = (bf16[64,8,8,64]{3,0,2,1:T(8,128)(2,1)S(1)}, bf16[64,8,8,64]{3,0,2,1:T(8,128)(2,1)S(1)}) fusion(f32[64,8,8,64]{3,2,1,0:T(8,128)S(1)} %reshape.55, f32[64]{0:T(128)S(1)} %mul.53, bf16[64,8,8,64]{0,3,2,1:T(8,128)(2,1)} %copy.58, bf16[3,3,64,64]{3,2,1,0:T(8,128)(2,1)S(1)} %bitcast.25), kind=kOutput, calls=%fused_computation.2 | convolution fusion | flops 256901120 | bytes 2695424 | tf_op jit(solution)/shard_map/conv_general_dilated | solution.py:46
  61.8 0.0 copy-start.5
  61.8 1.0 copy-done.5
  62.7 0.0 copy-done
  62.7 1.4 fusion.14
  64.2 0.2 all_to_all.26
  64.4 19.8 %all_to_all.32 = f32[32,1,1152]{2,1,0:T(1,128)S(1)} all-to-all(f32[32,1,1152]{2,1,0:T(1,128)S(1)} %all_to_all.26), channel_id=1, replica_groups=mesh['grp'=32,'slab'=32] {'slab'}, dimensions={0} | all-to-all | bytes 294912 | tf_op jit(solution)/shard_map/all_to_all | solution.py:21
  84.2 0.1 reduce_sum.28
  84.3 0.1 broadcast_in_dim.7
  84.4 20.3 %all_to_all.33 = f32[32,1,1152]{2,1,0:T(1,128)S(1)} all-to-all(f32[32,1,1152]{2,1,0:T(1,128)S(1)} %broadcast_in_dim.7), channel_id=1, replica_groups=mesh['grp'=32,'slab'=32] {'grp'}, dimensions={0} | all-to-all | bytes 294912 | tf_op jit(solution)/shard_map/all_to_all | solution.py:27
  104.7 0.1 reduce_sum.29
  104.8 0.7 broadcast_in_dim.8
  105.6 5.7 %all-to-all-start.4 = ((f32[32,1,1152]{2,1,0:T(1,128)}), f32[32,1,1152]{2,1,0:T(1,128)S(1)}, u32[]{:S(2)}, u32[]{:S(2)}) async-start(f32[32,1,1152]{2,1,0:T(1,128)} %broadcast_in_dim.8), calls=%async_computation.4 | async-start | bytes 294912 | tf_op jit(solution)/shard_map/all_to_all | solution.py:27
  111.3 0.7 copy.51
  112.0 0.6 reshape.53
  112.6 0.6 convolution_convert_fusion
  113.2 0.0 copy-start.6
  113.2 1.5 copy.53
  114.8 9.1 %all-to-all-done.4 = f32[32,1,1152]{2,1,0:T(1,128)S(1)} async-done(((f32[32,1,1152]{2,1,0:T(1,128)}), f32[32,1,1152]{2,1,0:T(1,128)S(1)}, u32[]{:S(2)}, u32[]{:S(2)}) %all-to-all-start.4) | async-done | bytes 147488 | tf_op jit(solution)/shard_map/all_to_all | solution.py:27
  123.9 4.5 %all-to-all-start = ((bf16[64,2,8,512]{3,2,1,0:T(8,128)(2,1)}), bf16[64,2,8,512]{3,2,1,0:T(8,128)(2,1)S(1)}, u32[]{:S(2)}, u32[]{:S(2)}) async-start(bf16[64,2,8,512]{3,2,1,0:T(8,128)(2,1)} %copy.53), calls=%async_computation | async-start | bytes 2097152 | tf_op jit(solution)/shard_map/all_to_all | solution.py:120
  128.3 0.0 copy-done.6
  128.3 2.6 %multiply_convert_fusion = bf16[64,8,8,64]{3,0,2,1:T(8,128)(2,1)S(1)} fusion(bf16[64,8,8,64]{3,0,2,1:T(8,128)(2,1)S(1)} %copy-done.6, bf16[3,3,64,64]{3,2,1,0:T(8,128)(2,1)S(1)} %bitcast.26, f32[64]{0:T(128)S(1)} %mul.53), kind=kOutput, calls=%fused_computation.3 | convolution fusion | flops 254279680 | bytes 1122560 | tf_op jit(solution)/shard_map/conv_general_dilated | solution.py:58
  130.9 0.7 copy.57
  131.6 1.4 reshape.54
  133.0 0.4 multiply_reduce_fusion
  133.4 0.1 mul.59
  133.5 0.8 copy.61
  134.4 23.4 %all-to-all-done = bf16[64,2,8,512]{3,2,1,0:T(8,128)(2,1)S(1)} async-done(((bf16[64,2,8,512]{3,2,1,0:T(8,128)(2,1)}), bf16[64,2,8,512]{3,2,1,0:T(8,128)(2,1)S(1)}, u32[]{:S(2)}, u32[]{:S(2)}) %all-to-all-start) | async-done | bytes 1048608 | tf_op jit(solution)/shard_map/all_to_all | solution.py:120
  157.8 1.0 copy.74
  (3 shorter events, 0.0 us)
Async XLA Ops:
  0.6 23.4 %copy-start.3 = (s32[32]{0:T(128)S(1)}, s32[32]{0:T(128)}, u32[]{:S(2)}) copy-start(s32[32]{0:T(128)} %param.8) | copy-start | bytes 388
  0.6 23.6 %copy-start.2 = (bf16[576,64]{0,1:T(8,128)(2,1)S(1)}, bf16[576,64]{0,1:T(8,128)(2,1)}, u32[]{:S(2)}) copy-start(bf16[576,64]{0,1:T(8,128)(2,1)} %param.6) | copy-start | bytes 221188
  0.7 23.8 %copy-start.1 = (bf16[32,2,8,512]{3,2,1,0:T(8,128)(2,1)S(1)}, bf16[32,2,8,512]{3,2,1,0:T(8,128)(2,1)}, u32[]{:S(2)}) copy-start(bf16[32,2,8,512]{3,2,1,0:T(8,128)(2,1)} %param.5) | copy-start | bytes 1572868
  0.7 53.4 %all-to-all-start.1 = ((bf16[64,2,8,512]{3,2,1,0:T(8,128)(2,1)}), bf16[64,2,8,512]{3,2,1,0:T(8,128)(2,1)S(1)}, u32[]{:S(2)}, u32[]{:S(2)}) async-start(bf16[64,2,8,512]{3,2,1,0:T(8,128)(2,1)} %param.9), calls=%async_computation.1 | async-start | bytes 2097152 | tf_op jit(solution)/shard_map/all_to_all | solution.py:111
  24.1 2.9 %copy-start.4 = (s32[32,1]{0,1:T(1,128)S(1)}, s32[32,1]{0,1:T(1,128)}, u32[]{:S(2)}) copy-start(s32[32,1]{0,1:T(1,128)} %param.7) | copy-start | bytes 388
  56.4 6.4 %copy-start = (bf16[64,8,8,64]{0,3,2,1:T(8,128)(2,1)S(1)}, bf16[64,8,8,64]{0,3,2,1:T(8,128)(2,1)}, u32[]{:S(2)}) copy-start(bf16[64,8,8,64]{0,3,2,1:T(8,128)(2,1)} %copy.58) | copy-start | bytes 1572868
  61.8 1.0 copy-start.5
  105.6 18.3 %all-to-all-start.4 = ((f32[32,1,1152]{2,1,0:T(1,128)}), f32[32,1,1152]{2,1,0:T(1,128)S(1)}, u32[]{:S(2)}, u32[]{:S(2)}) async-start(f32[32,1,1152]{2,1,0:T(1,128)} %broadcast_in_dim.8), calls=%async_computation.4 | async-start | bytes 294912 | tf_op jit(solution)/shard_map/all_to_all | solution.py:27
  113.2 15.1 %copy-start.6 = (bf16[64,8,8,64]{3,0,2,1:T(8,128)(2,1)S(1)}, bf16[64,8,8,64]{3,0,2,1:T(8,128)(2,1)}, u32[]{:S(2)}) copy-start(bf16[64,8,8,64]{3,0,2,1:T(8,128)(2,1)} %copy-done.5) | copy-start | bytes 1572868
  123.9 34.0 %all-to-all-start = ((bf16[64,2,8,512]{3,2,1,0:T(8,128)(2,1)}), bf16[64,2,8,512]{3,2,1,0:T(8,128)(2,1)S(1)}, u32[]{:S(2)}, u32[]{:S(2)}) async-start(bf16[64,2,8,512]{3,2,1,0:T(8,128)(2,1)} %copy.53), calls=%async_computation | async-start | bytes 2097152 | tf_op jit(solution)/shard_map/all_to_all | solution.py:120
where the time goes:
time: 162 us; the launch traced here: 159 us
  waiting for transfers between devices  59.4 us (37%)
  blocking collectives  40.2 us (25%)
  starting transfers between devices  33.6 us (21%)
  local copies, waits for them, and re-layouts  12.7 us (8%)
  matrix products  11.3 us (7%)
    all_to_all x1, waiting for transfers between devices, local(): lax.all_to_all(cotangent, 'slab', split_axis=0, concat_axis=0, tiled=True)  26.9 us
    all_to_all x1, waiting for transfers between devices, local(): lax.all_to_all(outgoing, 'slab', split_axis=0, concat_axis=0, tiled=True)  23.4 us
    all_to_all x1, starting transfers between devices, local(): lax.all_to_all(cotangent, 'slab', split_axis=0, concat_axis=0, tiled=True)  23.4 us
    all_to_all x1, blocking collectives, sent_to_all(): lax.all_to_all(jnp.broadcast_to(x[None], (size, *x.shape)), axis, 0, 0, t...  20.3 us
    all_to_all x1, blocking collectives, sent_and_summed(): pieces = lax.all_to_all(cut_along(x, dim, size), axis, 0, 0, tiled=True)  19.8 us
    all_to_all x1, waiting for transfers between devices, sent_to_all(): lax.all_to_all(jnp.broadcast_to(x[None], (size, *x.shape)), axis, 0, 0, t...  9.09 us
    all_to_all x1, starting transfers between devices, sent_to_all(): lax.all_to_all(jnp.broadcast_to(x[None], (size, *x.shape)), axis, 0, 0, t...  5.75 us
    conv_general_dilated x1, matrix products, conv_forward(): lax.conv_general_dilated(planes, kernel, (1, 1), ((1, 1), (1, 1)), dimens...  5.37 us
  transfers between devices with their start and end apart: 3, of which 3 were waited for; matrix products, arithmetic and copies ran while one was open for 8% of the time, Pallas kernels for 0%

commit v1 on v0

--- a/solution.py
+++ b/solution.py
@@ -118,9 +118,7 @@
         "sk,kdhx->sdhx", placer, act_tiles, preferred_element_type=jnp.float32
     ).astype(jnp.bfloat16)
     activations = lax.all_to_all(outgoing, "slab", split_axis=0, concat_axis=0, tiled=True)
-    share = sent_and_summed(wgrad.reshape(-1), "slab", 0)
-    share = over_copies(share, "grp")
-    summed = gathered_copies(share, "slab", 0).reshape(9 * C, C)
+    summed = lax.psum(wgrad, ("grp", "slab"))
     scale = 1.0 / math.sqrt(per_owner * n_group * n_slab * TD * TH * TW)
     return (activations, input_grad, summed * scale)
 

time: 162 us -> 379 us (2.34)
  waiting for transfers between devices: 59.4 us -> 306 us
  blocking collectives: 40.2 us -> 0 us
  between operations: 0.87 us -> 14.2 us
    psum x0 -> x1, waiting for transfers between devices: none -> 279 us  [local(): summed = lax.psum(wgrad, ('grp', 'slab'))]
    all_to_all x2 -> x0, blocking collectives: 40.2 us -> none  [the longest x1 20.3 us: sent_to_all(): lax.all_to_all(jnp.broadcast_to(x[None], (size, *x.shape)), axis, 0, 0, t...]
    all_to_all x1, waiting for transfers between devices: 23.4 us -> 0.01 us  [local(): lax.all_to_all(outgoing, 'slab', split_axis=0, concat_axis=0, tiled=True)]
    all_to_all x1 -> x0, waiting for transfers between devices: 9.09 us -> none  [sent_to_all(): lax.all_to_all(jnp.broadcast_to(x[None], (size, *x.shape)), axis, 0, 0, t...]
    all_to_all x1 -> x0, starting transfers between devices: 5.75 us -> none  [sent_to_all(): lax.all_to_all(jnp.broadcast_to(x[None], (size, *x.shape)), axis, 0, 0, t...]
  transfers between devices with their start and end apart: 3 -> 3, of which waited for: 3 -> 2; matrix products, arithmetic and copies ran while one was open for 8% -> 4% of each run, Pallas kernels for 0% -> 0%
where the time goes in v1:
time: 379 us
  waiting for transfers between devices  306 us (81%)
  starting transfers between devices  31.1 us (8%)
  matrix products  14.8 us (4%)
  between operations  14.2 us (4%)
  local copies, waits for them, and re-layouts  10.6 us (3%)
    psum x1, waiting for transfers between devices, local(): summed = lax.psum(wgrad, ('grp', 'slab'))  279 us
    all_to_all x1, waiting for transfers between devices, local(): lax.all_to_all(cotangent, 'slab', split_axis=0, concat_axis=0, tiled=True)  26.9 us
    all_to_all x1, starting transfers between devices, local(): lax.all_to_all(cotangent, 'slab', split_axis=0, concat_axis=0, tiled=True)  23.4 us
  transfers between devices with their start and end apart: 3, of which 2 were waited for; matrix products, arithmetic and copies ran while one was open for 4% of the time, Pallas kernels for 0%

profile of v1, /device:TPU:1, one launch (start us, length us, event | category | flops | bytes accessed | tf_op | source)
XLA Modules:
  0.0 378.8 jit_solution(12096188087528392496)
XLA Ops:
  7.2 0.0 copy-start.3
  7.2 0.0 copy-start.2
  7.2 0.0 copy-start.1
  7.2 23.4 %all-to-all-start.1 = ((bf16[64,2,8,512]{3,2,1,0:T(8,128)(2,1)}), bf16[64,2,8,512]{3,2,1,0:T(8,128)(2,1)S(1)}, u32[]{:S(2)}, u32[]{:S(2)}) async-start(bf16[64,2,8,512]{3,2,1,0:T(8,128)(2,1)} %param.9), calls=%async_computation.1 | async-start | bytes 2097152 | tf_op jit(solution)/shard_map/all_to_all | solution.py:111
  30.6 0.0 copy-done.3
  30.6 0.0 copy-start.4
  30.6 0.1 broadcast_in_dim.2
  30.7 0.1 mul.50
  30.8 0.0 copy-done.2
  30.8 0.1 copy.37
  31.0 0.0 copy-done.1
  31.0 0.5 reshape.36
  31.5 2.0 copy.46
  33.5 0.0 copy-done.4
  33.5 0.2 convert_reduce_fusion
  33.7 26.9 %all-to-all-done.1 = bf16[64,2,8,512]{3,2,1,0:T(8,128)(2,1)S(1)} async-done(((bf16[64,2,8,512]{3,2,1,0:T(8,128)(2,1)}), bf16[64,2,8,512]{3,2,1,0:T(8,128)(2,1)S(1)}, u32[]{:S(2)}, u32[]{:S(2)}) %all-to-all-start.1) | async-done | bytes 1048608 | tf_op jit(solution)/shard_map/all_to_all | solution.py:111
  60.6 1.3 fusion.2
  61.9 0.6 copy.43
  62.5 0.4 reshape.41
  62.9 6.5 %fusion.1 = (bf16[64,8,8,64]{3,0,2,1:T(8,128)(2,1)}, bf16[64,8,8,64]{3,0,2,1:T(8,128)(2,1)S(1)}) fusion(f32[64,8,8,64]{3,2,1,0:T(8,128)S(1)} %reshape.41, f32[64]{0:T(128)S(1)} %mul.50, bf16[64,8,8,64]{0,3,2,1:T(8,128)(2,1)} %copy.46, bf16[3,3,64,64]{3,2,1,0:T(8,128)(2,1)S(1)} %bitcast.25), kind=kOutput, calls=%fused_computation.2 | convolution fusion | flops 256901120 | bytes 2695424 | tf_op jit(solution)/shard_map/conv_general_dilated | solution.py:46
  69.4 0.7 copy.39
  70.1 0.6 reshape.38
  70.7 0.6 convolution_convert_fusion
  71.3 0.0 copy-start
  71.3 1.5 copy.41
  72.8 7.5 %all-to-all-start = ((bf16[64,2,8,512]{3,2,1,0:T(8,128)(2,1)}), bf16[64,2,8,512]{3,2,1,0:T(8,128)(2,1)S(1)}, u32[]{:S(2)}, u32[]{:S(2)}) async-start(bf16[64,2,8,512]{3,2,1,0:T(8,128)(2,1)} %copy.41), calls=%async_computation | async-start | bytes 2097152 | tf_op jit(solution)/shard_map/all_to_all | solution.py:120
  80.3 0.2 all-reduce.2.cloned.1.call-start
  80.6 0.0 copy-done
  80.6 2.7 fusion.14
  83.2 0.8 copy.47
  84.0 0.0 all-reduce.2.cloned.1.call-update
  84.1 3.8 %multiply_convert_fusion = bf16[64,8,8,64]{3,0,2,1:T(8,128)(2,1)S(1)} fusion(bf16[64,8,8,64]{3,0,2,1:T(8,128)(2,1)} %get-tuple-element.9, bf16[3,3,64,64]{3,2,1,0:T(8,128)(2,1)S(1)} %bitcast.26, f32[64]{0:T(128)S(1)} %mul.50), kind=kOutput, calls=%fused_computation.3 | convolution fusion | flops 254279680 | bytes 1122560 | tf_op jit(solution)/shard_map/conv_general_dilated | solution.py:58
  87.9 0.7 copy.45
  88.6 1.4 reshape.39
  90.0 279.3 %all-reduce.2.cloned.1.call-done = f32[576,64]{0,1:T(8,128)} async-done(((f32[576,64]{0,1:T(8,128)}), f32[576,64]{0,1:T(8,128)}) %all-reduce.2.cloned.1.call-update) | async-done | bytes 147472 | tf_op jit(solution)/shard_map/psum | solution.py:121
  369.3 1.6 broadcast_multiply_fusion
  370.9 0.0 all-to-all-done
  370.9 1.0 copy.60
  (3 shorter events, 0.0 us)
Async XLA Ops:
  7.2 23.4 %copy-start.3 = (s32[32]{0:T(128)S(1)}, s32[32]{0:T(128)}, u32[]{:S(2)}) copy-start(s32[32]{0:T(128)} %param.8) | copy-start | bytes 388
  7.2 23.6 %copy-start.2 = (bf16[576,64]{0,1:T(8,128)(2,1)S(1)}, bf16[576,64]{0,1:T(8,128)(2,1)}, u32[]{:S(2)}) copy-start(bf16[576,64]{0,1:T(8,128)(2,1)} %param.6) | copy-start | bytes 221188
  7.2 23.8 %copy-start.1 = (bf16[32,2,8,512]{3,2,1,0:T(8,128)(2,1)S(1)}, bf16[32,2,8,512]{3,2,1,0:T(8,128)(2,1)}, u32[]{:S(2)}) copy-start(bf16[32,2,8,512]{3,2,1,0:T(8,128)(2,1)} %param.5) | copy-start | bytes 1572868
  7.2 53.4 %all-to-all-start.1 = ((bf16[64,2,8,512]{3,2,1,0:T(8,128)(2,1)}), bf16[64,2,8,512]{3,2,1,0:T(8,128)(2,1)S(1)}, u32[]{:S(2)}, u32[]{:S(2)}) async-start(bf16[64,2,8,512]{3,2,1,0:T(8,128)(2,1)} %param.9), calls=%async_computation.1 | async-start | bytes 2097152 | tf_op jit(solution)/shard_map/all_to_all | solution.py:111
  30.6 2.9 copy-start.4
  71.3 9.3 %copy-start = (bf16[64,8,8,64]{0,3,2,1:T(8,128)(2,1)S(1)}, bf16[64,8,8,64]{0,3,2,1:T(8,128)(2,1)}, u32[]{:S(2)}) copy-start(bf16[64,8,8,64]{0,3,2,1:T(8,128)(2,1)} %copy.46) | copy-start | bytes 1572868
  72.8 298.1 %all-to-all-start = ((bf16[64,2,8,512]{3,2,1,0:T(8,128)(2,1)}), bf16[64,2,8,512]{3,2,1,0:T(8,128)(2,1)S(1)}, u32[]{:S(2)}, u32[]{:S(2)}) async-start(bf16[64,2,8,512]{3,2,1,0:T(8,128)(2,1)} %copy.41), calls=%async_computation | async-start | bytes 2097152 | tf_op jit(solution)/shard_map/all_to_all | solution.py:120
  80.3 289.0 %all-reduce.2.cloned.1.call-start = ((), (), s32[]{:S(2)}) async-start(), calls=%async_computation.2 | async-start | bytes 327680 | tf_op jit(solution)/shard_map/psum | solution.py:121
Sparse Core Ops, SparseCore 0:
  86.5 282.8 all-reduce.1

commit v2 on v0

--- a/solution.py
+++ b/solution.py
@@ -117,8 +117,18 @@
     outgoing = jnp.einsum(
         "sk,kdhx->sdhx", placer, act_tiles, preferred_element_type=jnp.float32
     ).astype(jnp.bfloat16)
-    activations = lax.all_to_all(outgoing, "slab", split_axis=0, concat_axis=0, tiled=True)
-    share = sent_and_summed(wgrad.reshape(-1), "slab", 0)
+    flat_w = wgrad.reshape(n_slab, -1)
+    high = flat_w.astype(jnp.bfloat16)
+    low = (flat_w - high.astype(jnp.float32)).astype(jnp.bfloat16)
+    act_rows = outgoing.reshape(n_slab, -1)
+    act_width = act_rows.shape[1]
+    share_width = flat_w.shape[1]
+    payload = jnp.concatenate([act_rows, high, low], axis=1)
+    arrived = lax.all_to_all(payload, "slab", split_axis=0, concat_axis=0, tiled=True)
+    activations = arrived[:, :act_width].reshape(outgoing.shape)
+    got_high = arrived[:, act_width : act_width + share_width].astype(jnp.float32)
+    got_low = arrived[:, act_width + share_width :].astype(jnp.float32)
+    share = jnp.sum(got_high, axis=0) + jnp.sum(got_low, axis=0)
     share = over_copies(share, "grp")
     summed = gathered_copies(share, "slab", 0).reshape(9 * C, C)
     scale = 1.0 / math.sqrt(per_owner * n_group * n_slab * TD * TH * TW)

time: 162 us -> 163 us (level); the launches traced: 159 us -> 162 us
  waiting for transfers between devices: 59.4 us -> 32 us
  blocking collectives: 40.2 us -> 63.7 us
  local copies, waits for them, and re-layouts: 12.7 us -> 18.1 us
  matrix products: 11.3 us -> 14.7 us
  starting transfers between devices: 33.6 us -> 30.4 us
    all_to_all x1, blocking collectives: 19.8 us -> 43.6 us  [local(): lax.all_to_all(payload, 'slab', split_axis=0, concat_axis=0, tiled=True)]
    all_to_all x1 -> x0, waiting for transfers between devices: 23.4 us -> none  [local(): lax.all_to_all(outgoing, 'slab', split_axis=0, concat_axis=0, tiled=True)]
    all_to_all x1 -> x0, starting transfers between devices: 4.47 us -> none  [local(): lax.all_to_all(outgoing, 'slab', split_axis=0, concat_axis=0, tiled=True)]
    all_to_all x1, waiting for transfers between devices: 9.09 us -> 5.21 us  [sent_to_all(): lax.all_to_all(jnp.broadcast_to(x[None], (size, *x.shape)), axis, 0, 0, t...]
    unnamed x17 -> x23, local copies, waits for them, and re-layouts: 2.93 us -> 6.79 us
    reshape x0 -> x2, local copies, waits for them, and re-layouts: none -> 2.02 us  [the longest x1 1.31 us: local(): activations = arrived[:, :act_width].reshape(outgoing.shape)]
    all_to_all x0 -> x2, other arithmetic: none -> 1.64 us  [local(): lax.all_to_all(payload, 'slab', split_axis=0, concat_axis=0, tiled=True)]
  transfers between devices with their start and end apart: 3 -> 2, of which waited for: 3 -> 2; matrix products, arithmetic and copies ran while one was open for 8% -> 6% of each run, Pallas kernels for 0% -> 0%
where the time goes in v2:
time: 163 us; the launch traced here: 162 us
  blocking collectives  63.7 us (39%)
  waiting for transfers between devices  32 us (20%)
  starting transfers between devices  30.4 us (19%)
  local copies, waits for them, and re-layouts  18.1 us (11%)
  matrix products  14.7 us (9%)
  other arithmetic  2.4 us (1%)
    all_to_all x1, blocking collectives, local(): lax.all_to_all(payload, 'slab', split_axis=0, concat_axis=0, tiled=True)  43.6 us
    all_to_all x1, waiting for transfers between devices, local(): lax.all_to_all(cotangent, 'slab', split_axis=0, concat_axis=0, tiled=True)  26.8 us
    all_to_all x1, starting transfers between devices, local(): lax.all_to_all(cotangent, 'slab', split_axis=0, concat_axis=0, tiled=True)  23.4 us
    all_to_all x1, blocking collectives, sent_to_all(): lax.all_to_all(jnp.broadcast_to(x[None], (size, *x.shape)), axis, 0, 0, t...  20 us
    all_to_all x1, starting transfers between devices, sent_to_all(): lax.all_to_all(jnp.broadcast_to(x[None], (size, *x.shape)), axis, 0, 0, t...  6.95 us
    unnamed x23, local copies, waits for them, and re-layouts  6.79 us
    conv_general_dilated x1, matrix products, conv_forward(): lax.conv_general_dilated(planes, kernel, (1, 1), ((1, 1), (1, 1)), dimens...  6.39 us
    all_to_all x1, waiting for transfers between devices, sent_to_all(): lax.all_to_all(jnp.broadcast_to(x[None], (size, *x.shape)), axis, 0, 0, t...  5.21 us
  transfers between devices with their start and end apart: 2, of which 2 were waited for; matrix products, arithmetic and copies ran while one was open for 6% of the time, Pallas kernels for 0%

profile of v2, /device:TPU:1, one launch (start us, length us, event | category | flops | bytes accessed | tf_op | source)
XLA Modules:
  0.0 162.2 jit_solution(16527962856971493389)
XLA Ops:
  0.6 0.0 copy-start.3
  0.6 23.4 %all-to-all-start = ((bf16[64,2,8,512]{3,2,1,0:T(8,128)(2,1)}), bf16[64,2,8,512]{3,2,1,0:T(8,128)(2,1)S(1)}, u32[]{:S(2)}, u32[]{:S(2)}) async-start(bf16[64,2,8,512]{3,2,1,0:T(8,128)(2,1)} %param.9), calls=%async_computation | async-start | bytes 2097152 | tf_op jit(solution)/shard_map/all_to_all | solution.py:111
  24.1 0.0 copy-done.3
  24.1 0.0 copy-start.6
  24.1 0.0 copy-start.7
  24.1 0.0 copy-start.8
  24.1 0.5 reshape.61
  24.6 2.0 %copy.68 = bf16[64,8,8,64]{0,3,2,1:T(8,128)(2,1)} copy(bf16[64,8,8,64]{3,2,1,0:T(8,128)(2,1)S(1)} %reshape.61) | data formatting | bytes 1048576 | tf_op jit(solution)/shard_map/reshape | solution.py:81
  26.6 0.0 copy-done.6
  26.6 0.1 copy.60
  26.7 0.0 copy-done.7
  26.8 0.0 copy-start.4
  26.8 0.1 broadcast_in_dim.6
  26.9 0.1 mul.53
  27.0 0.0 copy-done.8
  27.0 0.2 convert_reduce_fusion.2
  27.2 26.8 %all-to-all-done = bf16[64,2,8,512]{3,2,1,0:T(8,128)(2,1)S(1)} async-done(((bf16[64,2,8,512]{3,2,1,0:T(8,128)(2,1)}), bf16[64,2,8,512]{3,2,1,0:T(8,128)(2,1)S(1)}, u32[]{:S(2)}, u32[]{:S(2)}) %all-to-all-start) | async-done | bytes 1048608 | tf_op jit(solution)/shard_map/all_to_all | solution.py:111
  54.0 1.3 fusion.2
  55.3 0.6 copy.66
  55.9 0.4 reshape.67
  56.4 0.0 copy-done.4
  56.4 0.0 copy-start.2
  56.4 6.4 %multiply_convert_fusion.1 = (bf16[64,8,8,64]{3,0,2,1:T(8,128)(2,1)S(1)}, bf16[64,8,8,64]{3,0,2,1:T(8,128)(2,1)}) fusion(f32[64]{0:T(128)S(1)} %mul.53, f32[64,8,8,64]{3,2,1,0:T(8,128)S(1)} %reshape.67, bf16[64,8,8,64]{0,3,2,1:T(8,128)(2,1)} %copy.68, bf16[3,3,64,64]{3,2,1,0:T(8,128)(2,1)S(1)} %bitcast.34), kind=kOutput, calls=%fused_computation.4 | convolution fusion | flops 256901120 | bytes 2695424 | tf_op jit(solution)/shard_map/conv_general_dilated | solution.py:46
  62.8 0.0 copy-done.2
  62.8 2.7 %fusion.14 = f32[3,3,64,64]{3,2,1,0:T(8,128)S(1)} fusion(bf16[64,8,8,64]{0,3,2,1:T(8,128)(2,1)S(1)} %copy-done.2, bf16[64,8,8,64]{3,0,2,1:T(8,128)(2,1)} %get-tuple-element.23), kind=kOutput, calls=%fused_computation.29 | convolution fusion | flops 253755392 | bytes 1196032 | tf_op jit(solution)/shard_map/conv_general_dilated | solution.py:69
  65.4 0.1 reshape_reshape.4
  65.6 0.7 copy.62
  66.3 0.6 reshape.63
  66.9 0.6 convolution_convert_fusion
  67.5 0.6 copy.64
  68.0 0.7 reshape.64
  68.8 0.1 maximum_bitcast_fusion
  68.8 0.5 broadcast.22
  69.4 1.6 reduce.3
  70.9 0.4 reshape.70
  71.3 43.6 %all_to_all.29 = bf16[32,2,9344]{2,1,0:T(2,128)(2,1)} all-to-all(bf16[32,2,9344]{2,1,0:T(2,128)(2,1)S(1)} %reshape.70), channel_id=1, replica_groups=mesh['grp'=32,'slab'=32] {'slab'}, dimensions={0} | all-to-all | bytes 2392064 | tf_op jit(solution)/shard_map/all_to_all | solution.py:127
  114.9 4.3 %reshape.71 = bf16[32,1,18688]{2,1,0:T(2,128)(2,1)S(1)} reshape(bf16[32,2,9344]{2,1,0:T(2,128)(2,1)} %all_to_all.29) | data formatting | bytes 2392064
  119.2 0.0 copy-start.5
  119.2 0.1 copy.86
  119.4 0.0 copy-start
  119.4 1.0 copy-done
  120.5 0.1 broadcast_in_dim.7
  120.5 20.0 %all_to_all.30 = f32[32,1,1152]{2,1,0:T(1,128)S(1)} all-to-all(f32[32,1,1152]{2,1,0:T(1,128)S(1)} %broadcast_in_dim.7), channel_id=1, replica_groups=mesh['grp'=32,'slab'=32] {'grp'}, dimensions={0} | all-to-all | bytes 294912 | tf_op jit(solution)/shard_map/all_to_all | solution.py:27
  140.6 0.1 reduce_sum.39
  140.7 0.7 broadcast_in_dim.8
  141.4 7.0 %all-to-all-start.3 = ((f32[32,1,1152]{2,1,0:T(1,128)}), f32[32,1,1152]{2,1,0:T(1,128)S(1)}, u32[]{:S(2)}, u32[]{:S(2)}) async-start(f32[32,1,1152]{2,1,0:T(1,128)} %broadcast_in_dim.8), calls=%async_computation.3 | async-start | bytes 294912 | tf_op jit(solution)/shard_map/all_to_all | solution.py:27
  148.4 0.0 copy-done.5
  148.4 3.8 %multiply_convert_fusion = bf16[64,8,8,64]{3,0,2,1:T(8,128)(2,1)S(1)} fusion(bf16[64,8,8,64]{3,0,2,1:T(8,128)(2,1)} %get-tuple-element.23, bf16[3,3,64,64]{3,2,1,0:T(8,128)(2,1)S(1)} %bitcast.35, f32[64]{0:T(128)S(1)} %mul.53), kind=kOutput, calls=%fused_computation.3 | convolution fusion | flops 254279680 | bytes 1122560 | tf_op jit(solution)/shard_map/conv_general_dilated | solution.py:58
  152.2 0.0 copy-start.1
  152.2 0.7 copy.70
  152.9 1.4 reshape.66
  154.3 0.0 copy-done.1
  154.3 0.1 slice.12
  154.4 1.3 reshape.65
  155.7 5.2 %all-to-all-done.3 = f32[32,1,1152]{2,1,0:T(1,128)S(1)} async-done(((f32[32,1,1152]{2,1,0:T(1,128)}), f32[32,1,1152]{2,1,0:T(1,128)S(1)}, u32[]{:S(2)}, u32[]{:S(2)}) %all-to-all-start.3) | async-done | bytes 147488 | tf_op jit(solution)/shard_map/all_to_all | solution.py:27
  160.9 0.4 multiply_reduce_fusion
  161.3 0.1 mul.59
  161.4 0.8 copy.72
  (6 shorter events, 0.1 us)
Async XLA Ops:
  0.6 23.4 %copy-start.3 = (bf16[32,2,8,512]{3,2,1,0:T(8,128)(2,1)S(1)}, bf16[32,2,8,512]{3,2,1,0:T(8,128)(2,1)}, u32[]{:S(2)}) copy-start(bf16[32,2,8,512]{3,2,1,0:T(8,128)(2,1)} %param.5) | copy-start | bytes 1572868
  0.6 53.4 %all-to-all-start = ((bf16[64,2,8,512]{3,2,1,0:T(8,128)(2,1)}), bf16[64,2,8,512]{3,2,1,0:T(8,128)(2,1)S(1)}, u32[]{:S(2)}, u32[]{:S(2)}) async-start(bf16[64,2,8,512]{3,2,1,0:T(8,128)(2,1)} %param.9), calls=%async_computation | async-start | bytes 2097152 | tf_op jit(solution)/shard_map/all_to_all | solution.py:111
  24.1 2.5 %copy-start.6 = (bf16[576,64]{0,1:T(8,128)(2,1)S(1)}, bf16[576,64]{0,1:T(8,128)(2,1)}, u32[]{:S(2)}) copy-start(bf16[576,64]{0,1:T(8,128)(2,1)} %param.6) | copy-start | bytes 221188
  24.1 2.7 %copy-start.7 = (s32[32]{0:T(128)S(1)}, s32[32]{0:T(128)}, u32[]{:S(2)}) copy-start(s32[32]{0:T(128)} %param.8) | copy-start | bytes 388
  24.1 2.9 %copy-start.8 = (s32[32,1]{0,1:T(1,128)S(1)}, s32[32,1]{0,1:T(1,128)}, u32[]{:S(2)}) copy-start(s32[32,1]{0,1:T(1,128)} %param.7) | copy-start | bytes 388
  26.8 29.6 %copy-start.4 = (bf16[576,64]{1,0:T(8,128)(2,1)}, bf16[576,64]{1,0:T(8,128)(2,1)S(1)}, u32[]{:S(2)}) copy-start(bf16[576,64]{1,0:T(8,128)(2,1)S(1)} %copy.60) | copy-start | bytes 221188
  56.4 6.4 %copy-start.2 = (bf16[64,8,8,64]{0,3,2,1:T(8,128)(2,1)S(1)}, bf16[64,8,8,64]{0,3,2,1:T(8,128)(2,1)}, u32[]{:S(2)}) copy-start(bf16[64,8,8,64]{0,3,2,1:T(8,128)(2,1)} %copy.68) | copy-start | bytes 1572868
  119.2 29.1 %copy-start.5 = (bf16[576,64]{1,0:T(8,128)(2,1)S(1)}, bf16[576,64]{1,0:T(8,128)(2,1)}, u32[]{:S(2)}) copy-start(bf16[576,64]{1,0:T(8,128)(2,1)} %copy-done.4) | copy-start | bytes 221188
  119.4 1.0 copy-start
  141.4 19.5 %all-to-all-start.3 = ((f32[32,1,1152]{2,1,0:T(1,128)}), f32[32,1,1152]{2,1,0:T(1,128)S(1)}, u32[]{:S(2)}, u32[]{:S(2)}) async-start(f32[32,1,1152]{2,1,0:T(1,128)} %broadcast_in_dim.8), calls=%async_computation.3 | async-start | bytes 294912 | tf_op jit(solution)/shard_map/all_to_all | solution.py:27
  152.2 2.1 %copy-start.1 = (bf16[32,1,18688]{2,0,1:T(8,128)(2,1)S(1)}, bf16[32,1,18688]{2,0,1:T(8,128)(2,1)}, u32[]{:S(2)}) copy-start(bf16[32,1,18688]{2,0,1:T(8,128)(2,1)} %copy-done) | copy-start | bytes 3588100

commit v3 on v0

--- a/solution.py
+++ b/solution.py
@@ -76,23 +76,6 @@
     )
 
 
-def layer_local(tile_set, kernel, upstream, mask):
-    count = tile_set.shape[0]
-    planes = tile_set.reshape(count * TD, TH, TW, C)
-    pre = conv_forward(planes, kernel)
-    sig = jax.nn.sigmoid(pre)
-    act = (pre * sig).astype(jnp.bfloat16).reshape(count, TD, TH, TW * C)
-    slope = sig * (1.0 + pre * (1.0 - sig))
-    grad_pre = upstream.reshape(count * TD, TH, TW, C).astype(jnp.float32) * slope
-    plane_mask = jnp.repeat(mask, TD)
-    grad_pre = grad_pre * plane_mask[:, None, None, None]
-    grad_pre = grad_pre.astype(jnp.bfloat16)
-    back = conv_input_grad(grad_pre, kernel)
-    wgrad = conv_kernel_grad(planes, grad_pre).reshape(9 * C, C)
-    back = back * plane_mask[:, None, None, None]
-    return (act, back.astype(jnp.bfloat16).reshape(count, TD, TH, TW * C), wgrad)
-
-
 def local(tiles, conv_weight, assignment, occupancy, cotangent):
     n_slab = lax.axis_size("slab")
     n_group = lax.axis_size("grp")
@@ -109,16 +92,46 @@
     ).astype(jnp.bfloat16)
     kernel = conv_weight.reshape(3, 3, C, C)
     upstream_slots = lax.all_to_all(cotangent, "slab", split_axis=0, concat_axis=0, tiled=True)
+
+    count = per_owner
+    planes = tiles.reshape(count * TD, TH, TW, C)
+    pre = conv_forward(planes, kernel)
+    sig = jax.nn.sigmoid(pre)
+    act_tiles = (pre * sig).astype(jnp.bfloat16).reshape(count, TD, TH, TW * C)
+    slope = sig * (1.0 + pre * (1.0 - sig))
+    outgoing = jnp.einsum(
+        "sk,kdhx->sdhx", placer, act_tiles, preferred_element_type=jnp.float32
+    ).astype(jnp.bfloat16)
+    outgoing, slope = lax.optimization_barrier((outgoing, slope))
+
     upstream = jnp.einsum(
         "sk,sdhx->kdhx", placer, upstream_slots, preferred_element_type=jnp.float32
     ).astype(jnp.bfloat16)
     mask = occupancy.astype(jnp.float32)
-    act_tiles, input_grad, wgrad = layer_local(tiles, kernel, upstream, mask)
-    outgoing = jnp.einsum(
-        "sk,kdhx->sdhx", placer, act_tiles, preferred_element_type=jnp.float32
-    ).astype(jnp.bfloat16)
-    activations = lax.all_to_all(outgoing, "slab", split_axis=0, concat_axis=0, tiled=True)
-    share = sent_and_summed(wgrad.reshape(-1), "slab", 0)
+    plane_mask = jnp.repeat(mask, TD)
+    grad_pre = upstream.reshape(count * TD, TH, TW, C).astype(jnp.float32) * slope
+    grad_pre = grad_pre * plane_mask[:, None, None, None]
+    grad_pre = grad_pre.astype(jnp.bfloat16)
+    back = conv_input_grad(grad_pre, kernel)
+    wgrad = conv_kernel_grad(planes, grad_pre).reshape(9 * C, C)
+    back = back * plane_mask[:, None, None, None]
+    input_grad = back.astype(jnp.bfloat16).reshape(count, TD, TH, TW * C)
+
+    flat_w = wgrad.reshape(n_slab, -1)
+    high = lax.reduce_precision(flat_w, exponent_bits=8, mantissa_bits=7)
+    low = flat_w - high
+    share_width = flat_w.shape[1]
+    plane = TH * TW * C
+    extra = -(-2 * share_width // plane)
+    pair = jnp.concatenate([high, low], axis=1).astype(jnp.bfloat16)
+    pair = jnp.pad(pair, ((0, 0), (0, extra * plane - 2 * share_width)))
+    pair = pair.reshape(n_slab, extra, TH, TW * C)
+    act_rows = outgoing.reshape(n_slab, capacity * TD, TH, TW * C)
+    payload = jnp.concatenate([act_rows, pair], axis=1)
+    arrived = lax.all_to_all(payload, "slab", split_axis=0, concat_axis=0, tiled=True)
+    activations = arrived[:, : capacity * TD].reshape(outgoing.shape)
+    got = arrived[:, capacity * TD :].reshape(n_slab, -1)[:, : 2 * share_width].astype(jnp.float32)
+    share = jnp.sum(got[:, :share_width], axis=0) + jnp.sum(got[:, share_width:], axis=0)
     share = over_copies(share, "grp")
     summed = gathered_copies(share, "slab", 0).reshape(9 * C, C)
     scale = 1.0 / math.sqrt(per_owner * n_group * n_slab * TD * TH * TW)

time: 162 us -> 149 us (0.920); the launches traced: 159 us -> 149 us
  waiting for transfers between devices: 59.4 us -> 26.9 us
  blocking collectives: 40.2 us -> 65.7 us
  starting transfers between devices: 33.6 us -> 30.4 us
  other arithmetic: 0.79 us -> 3.85 us
    all_to_all x1, blocking collectives: 19.8 us -> 45.9 us  [local(): lax.all_to_all(payload, 'slab', split_axis=0, concat_axis=0, tiled=True)]
    all_to_all x1 -> x0, waiting for transfers between devices: 23.4 us -> none  [local(): lax.all_to_all(outgoing, 'slab', split_axis=0, concat_axis=0, tiled=True)]
    all_to_all x1, waiting for transfers between devices: 26.9 us -> 20.2 us  [local(): lax.all_to_all(cotangent, 'slab', split_axis=0, concat_axis=0, tiled=True)]
    all_to_all x1 -> x0, starting transfers between devices: 4.47 us -> none  [local(): lax.all_to_all(outgoing, 'slab', split_axis=0, concat_axis=0, tiled=True)]
    convert_element_type x0 -> x2, other arithmetic: none -> 2.96 us  [the longest x1 2.94 us: local(): grad_pre = grad_pre.astype(jnp.bfloat16)]
    all_to_all x1, waiting for transfers between devices: 9.09 us -> 6.73 us  [sent_to_all(): lax.all_to_all(jnp.broadcast_to(x[None], (size, *x.shape)), axis, 0, 0, t...]
    unnamed x17 -> x18, local copies, waits for them, and re-layouts: 2.93 us -> 1.16 us
    convert_element_type x5 -> x4, local copies, waits for them, and re-layouts: 3.94 us -> 2.39 us  [the longest x2 1.03 us: local(): upstream.reshape(count * TD, TH, TW, C).astype(jnp.float32) * slope]
  transfers between devices with their start and end apart: 3 -> 2, of which waited for: 3 -> 2; matrix products, arithmetic and copies ran while one was open for 8% -> 10% of each run, Pallas kernels for 0% -> 0%
where the time goes in v3:
time: 149 us
  blocking collectives  65.7 us (44%)
  starting transfers between devices  30.4 us (20%)
  waiting for transfers between devices  26.9 us (18%)
  local copies, waits for them, and re-layouts  11.2 us (8%)
  matrix products  9.88 us (7%)
  other arithmetic  3.85 us (3%)
    all_to_all x1, blocking collectives, local(): lax.all_to_all(payload, 'slab', split_axis=0, concat_axis=0, tiled=True)  45.9 us
    all_to_all x1, starting transfers between devices, local(): lax.all_to_all(cotangent, 'slab', split_axis=0, concat_axis=0, tiled=True)  23.4 us
    all_to_all x1, waiting for transfers between devices, local(): lax.all_to_all(cotangent, 'slab', split_axis=0, concat_axis=0, tiled=True)  20.2 us
    all_to_all x1, blocking collectives, sent_to_all(): lax.all_to_all(jnp.broadcast_to(x[None], (size, *x.shape)), axis, 0, 0, t...  19.9 us
    all_to_all x1, starting transfers between devices, sent_to_all(): lax.all_to_all(jnp.broadcast_to(x[None], (size, *x.shape)), axis, 0, 0, t...  6.97 us
    all_to_all x1, waiting for transfers between devices, sent_to_all(): lax.all_to_all(jnp.broadcast_to(x[None], (size, *x.shape)), axis, 0, 0, t...  6.73 us
    conv_general_dilated x1, matrix products, conv_forward(): lax.conv_general_dilated(planes, kernel, (1, 1), ((1, 1), (1, 1)), dimens...  3.97 us
  transfers between devices with their start and end apart: 2, of which 2 were waited for; matrix products, arithmetic and copies ran while one was open for 10% of the time, Pallas kernels for 0%

profile of v3, /device:TPU:1, one launch (start us, length us, event | category | flops | bytes accessed | tf_op | source)
XLA Modules:
  0.0 148.9 jit_solution(1464793231038620065)
XLA Ops:
  0.6 0.0 copy-start.3
  0.6 23.4 %all-to-all-start = ((bf16[64,2,8,512]{3,2,1,0:T(8,128)(2,1)}), bf16[64,2,8,512]{3,2,1,0:T(8,128)(2,1)S(1)}, u32[]{:S(2)}, u32[]{:S(2)}) async-start(bf16[64,2,8,512]{3,2,1,0:T(8,128)(2,1)} %param.9), calls=%async_computation | async-start | bytes 2097152 | tf_op jit(solution)/shard_map/all_to_all | solution.py:94
  24.1 0.0 copy-done.3
  24.1 0.0 copy-start.4
  24.1 0.5 reshape.65
  24.6 1.2 copy.55
  25.8 0.0 copy-done.4
  25.9 0.0 copy-start.1
  25.9 0.1 copy.47
  26.0 4.0 %add_multiply_fusion = (f32[64,8,8,64]{3,0,2,1:T(8,128)}, bf16[64,8,8,64]{3,0,2,1:T(8,128)(2,1)S(1)}) fusion(bf16[64,8,8,64]{0,3,2,1:T(8,128)(2,1)S(1)} %copy.55, bf16[3,3,64,64]{3,2,1,0:T(8,128)(2,1)S(1)} %bitcast.39), kind=kOutput, calls=%fused_computation.4 | convolution fusion | flops 256114688 | bytes 2170880 | tf_op jit(solution)/shard_map/conv_general_dilated | solution.py:46
  30.0 0.0 copy-done.1
  30.0 0.0 copy-start.5
  30.0 0.0 copy-start.6
  30.0 0.7 copy.49
  30.7 0.6 reshape.67
  31.3 0.0 copy-done.5
  31.3 0.0 copy-done.6
  31.3 0.2 convert_reduce_fusion
  31.5 0.6 convolution_convert_fusion
  32.1 0.1 broadcast_in_dim.6
  32.2 0.1 mul.53
  32.3 1.6 %copy.51 = bf16[64,2,8,512]{3,2,1,0:T(8,128)(2,1)} copy(bf16[64,2,8,512]{3,0,2,1:T(8,128)(2,1)S(1)} %convolution_convert_fusion) | data formatting | bytes 2097152 | tf_op jit(solution)/shard_map/optimization_barrier | solution.py:105
  33.8 20.2 %all-to-all-done = bf16[64,2,8,512]{3,2,1,0:T(8,128)(2,1)S(1)} async-done(((bf16[64,2,8,512]{3,2,1,0:T(8,128)(2,1)}), bf16[64,2,8,512]{3,2,1,0:T(8,128)(2,1)S(1)}, u32[]{:S(2)}, u32[]{:S(2)}) %all-to-all-start) | async-done | bytes 1048608 | tf_op jit(solution)/shard_map/all_to_all | solution.py:94
  54.0 1.3 fusion.2
  55.3 0.6 copy.53
  55.9 0.4 reshape.73
  56.4 0.0 copy-start.2
  56.4 2.9 %fusion.1 = bf16[64,8,8,64]{3,0,2,1:T(8,128)(2,1)S(1)} fusion(f32[64,8,8,64]{3,0,2,1:T(8,128)} %get-tuple-element.6, f32[64,8,8,64]{3,2,1,0:T(8,128)S(1)} %reshape.73, f32[64]{0:T(128)S(1)} %mul.53), kind=kLoop, calls=%fused_computation.2 | loop fusion | flops 786432 | bytes 2621696 | tf_op jit(solution)/shard_map/convert_element_type | solution.py:114
  59.3 0.0 copy-done.2
  59.3 0.0 copy-start
  59.3 1.4 fusion.18
  60.8 0.1 reshape_reshape.4
  61.0 0.1 copy.61
  61.0 0.0 copy-done
  61.1 0.1 pad_maximum_fusion
  61.2 45.9 %all_to_all.22 = bf16[32,5,8,512]{3,2,1,0:T(8,128)(2,1)S(1)} all-to-all(bf16[32,5,8,512]{3,2,1,0:T(8,128)(2,1)S(1)} %pad_maximum_fusion), channel_id=1, replica_groups=mesh['grp'=32,'slab'=32] {'slab'}, dimensions={0} | all-to-all | bytes 2621440 | tf_op jit(solution)/shard_map/all_to_all | solution.py:131
  107.1 0.1 copy.62
  107.2 0.1 broadcast_in_dim.7
  107.3 19.9 %all_to_all.23 = f32[32,1,1152]{2,1,0:T(1,128)S(1)} all-to-all(f32[32,1,1152]{2,1,0:T(1,128)S(1)} %broadcast_in_dim.7), channel_id=1, replica_groups=mesh['grp'=32,'slab'=32] {'grp'}, dimensions={0} | all-to-all | bytes 294912 | tf_op jit(solution)/shard_map/all_to_all | solution.py:27
  127.2 0.1 reduce_sum.39
  127.3 0.7 broadcast_in_dim.8
  128.0 7.0 %all-to-all-start.3 = ((f32[32,1,1152]{2,1,0:T(1,128)}), f32[32,1,1152]{2,1,0:T(1,128)S(1)}, u32[]{:S(2)}, u32[]{:S(2)}) async-start(f32[32,1,1152]{2,1,0:T(1,128)} %broadcast_in_dim.8), calls=%async_computation.3 | async-start | bytes 294912 | tf_op jit(solution)/shard_map/all_to_all | solution.py:27
  135.0 2.6 %multiply_convert_fusion = bf16[64,8,8,64]{3,0,2,1:T(8,128)(2,1)S(1)} fusion(bf16[64,8,8,64]{3,0,2,1:T(8,128)(2,1)S(1)} %fusion.1, bf16[3,3,64,64]{3,2,1,0:T(8,128)(2,1)S(1)} %bitcast.40, f32[64]{0:T(128)S(1)} %mul.53), kind=kOutput, calls=%fused_computation.3 | convolution fusion | flops 254279680 | bytes 1122560 | tf_op jit(solution)/shard_map/conv_general_dilated | solution.py:58
  137.6 0.7 copy.56
  138.3 1.4 reshape.71
  139.7 1.1 slice.20
  140.8 6.7 %all-to-all-done.3 = f32[32,1,1152]{2,1,0:T(1,128)S(1)} async-done(((f32[32,1,1152]{2,1,0:T(1,128)}), f32[32,1,1152]{2,1,0:T(1,128)S(1)}, u32[]{:S(2)}, u32[]{:S(2)}) %all-to-all-start.3) | async-done | bytes 147488 | tf_op jit(solution)/shard_map/all_to_all | solution.py:27
  147.5 0.4 multiply_reduce_fusion
  147.9 0.1 mul.59
  148.1 0.8 copy.58
  (9 shorter events, 0.1 us)
Async XLA Ops:
  0.6 23.4 %copy-start.3 = (bf16[32,2,8,512]{3,2,1,0:T(8,128)(2,1)S(1)}, bf16[32,2,8,512]{3,2,1,0:T(8,128)(2,1)}, u32[]{:S(2)}) copy-start(bf16[32,2,8,512]{3,2,1,0:T(8,128)(2,1)} %param.5) | copy-start | bytes 1572868
  0.6 53.4 %all-to-all-start = ((bf16[64,2,8,512]{3,2,1,0:T(8,128)(2,1)}), bf16[64,2,8,512]{3,2,1,0:T(8,128)(2,1)S(1)}, u32[]{:S(2)}, u32[]{:S(2)}) async-start(bf16[64,2,8,512]{3,2,1,0:T(8,128)(2,1)} %param.9), calls=%async_computation | async-start | bytes 2097152 | tf_op jit(solution)/shard_map/all_to_all | solution.py:94
  24.1 1.8 %copy-start.4 = (bf16[576,64]{0,1:T(8,128)(2,1)S(1)}, bf16[576,64]{0,1:T(8,128)(2,1)}, u32[]{:S(2)}) copy-start(bf16[576,64]{0,1:T(8,128)(2,1)} %param.6) | copy-start | bytes 221188
  25.9 4.1 %copy-start.1 = (bf16[64,8,8,64]{0,3,2,1:T(8,128)(2,1)}, bf16[64,8,8,64]{0,3,2,1:T(8,128)(2,1)S(1)}, u32[]{:S(2)}) copy-start(bf16[64,8,8,64]{0,3,2,1:T(8,128)(2,1)S(1)} %copy.55) | copy-start | bytes 1572868
  30.0 1.3 copy-start.5
  30.0 1.3 copy-start.6
  56.4 3.0 %copy-start.2 = (bf16[64,8,8,64]{0,3,2,1:T(8,128)(2,1)S(1)}, bf16[64,8,8,64]{0,3,2,1:T(8,128)(2,1)}, u32[]{:S(2)}) copy-start(bf16[64,8,8,64]{0,3,2,1:T(8,128)(2,1)} %copy-done.1) | copy-start | bytes 1572868
  59.3 1.7 %copy-start = (bf16[64,2,8,512]{3,2,1,0:T(8,128)(2,1)S(1)}, bf16[64,2,8,512]{3,2,1,0:T(8,128)(2,1)}, u32[]{:S(2)}) copy-start(bf16[64,2,8,512]{3,2,1,0:T(8,128)(2,1)} %copy.51) | copy-start | bytes 3145732
  128.0 19.5 %all-to-all-start.3 = ((f32[32,1,1152]{2,1,0:T(1,128)}), f32[32,1,1152]{2,1,0:T(1,128)S(1)}, u32[]{:S(2)}, u32[]{:S(2)}) async-start(f32[32,1,1152]{2,1,0:T(1,128)} %broadcast_in_dim.8), calls=%async_computation.3 | async-start | bytes 294912 | tf_op jit(solution)/shard_map/all_to_all | solution.py:27

commit v4 on v3

--- a/solution.py
+++ b/solution.py
@@ -104,9 +104,7 @@
     ).astype(jnp.bfloat16)
     outgoing, slope = lax.optimization_barrier((outgoing, slope))
 
-    upstream = jnp.einsum(
-        "sk,sdhx->kdhx", placer, upstream_slots, preferred_element_type=jnp.float32
-    ).astype(jnp.bfloat16)
+    upstream = jnp.take(upstream_slots, slot_ids, axis=0, mode="clip")
     mask = occupancy.astype(jnp.float32)
     plane_mask = jnp.repeat(mask, TD)
     grad_pre = upstream.reshape(count * TD, TH, TW, C).astype(jnp.float32) * slope

time: 149 us -> 151 us (1.013)
  local copies, waits for them, and re-layouts: 11.2 us -> 13.1 us
where the time goes in v4:
time: 151 us
  blocking collectives  65.8 us (44%)
  starting transfers between devices  30.4 us (20%)
  waiting for transfers between devices  27.8 us (18%)
  local copies, waits for them, and re-layouts  13.1 us (9%)
  matrix products  8.55 us (6%)
  other arithmetic  3.86 us (3%)
    all_to_all x1, blocking collectives, local(): lax.all_to_all(payload, 'slab', split_axis=0, concat_axis=0, tiled=True)  45.8 us
    all_to_all x1, starting transfers between devices, local(): lax.all_to_all(cotangent, 'slab', split_axis=0, concat_axis=0, tiled=True)  23.4 us
    all_to_all x1, waiting for transfers between devices, local(): lax.all_to_all(cotangent, 'slab', split_axis=0, concat_axis=0, tiled=True)  21.1 us
    all_to_all x1, blocking collectives, sent_to_all(): lax.all_to_all(jnp.broadcast_to(x[None], (size, *x.shape)), axis, 0, 0, t...  20 us
    all_to_all x1, starting transfers between devices, sent_to_all(): lax.all_to_all(jnp.broadcast_to(x[None], (size, *x.shape)), axis, 0, 0, t...  6.98 us
    all_to_all x1, waiting for transfers between devices, sent_to_all(): lax.all_to_all(jnp.broadcast_to(x[None], (size, *x.shape)), axis, 0, 0, t...  6.71 us
    conv_general_dilated x1, matrix products, conv_forward(): lax.conv_general_dilated(planes, kernel, (1, 1), ((1, 1), (1, 1)), dimens...  3.97 us
  transfers between devices with their start and end apart: 2, of which 2 were waited for; matrix products, arithmetic and copies ran while one was open for 10% of the time, Pallas kernels for 0%

profile of v4, /device:TPU:1, one launch (start us, length us, event | category | flops | bytes accessed | tf_op | source)
XLA Modules:
  0.0 150.5 jit_solution(10906289994799013692)
XLA Ops:
  0.6 0.0 copy-start.4
  0.6 23.4 %all-to-all-start = ((bf16[64,2,8,512]{3,2,1,0:T(8,128)(2,1)}), bf16[64,2,8,512]{3,2,1,0:T(8,128)(2,1)S(1)}, u32[]{:S(2)}, u32[]{:S(2)}) async-start(bf16[64,2,8,512]{3,2,1,0:T(8,128)(2,1)} %param.9), calls=%async_computation | async-start | bytes 2097152 | tf_op jit(solution)/shard_map/all_to_all | solution.py:94
  24.1 0.0 copy-done.4
  24.1 0.0 copy-start.5
  24.1 0.5 reshape.66
  24.6 1.2 copy.46
  25.8 0.0 copy-done.5
  25.9 0.0 copy-start
  25.9 0.1 copy.40
  26.0 4.0 %add_multiply_fusion = (f32[64,8,8,64]{3,0,2,1:T(8,128)}, bf16[64,8,8,64]{3,0,2,1:T(8,128)(2,1)S(1)}) fusion(bf16[64,8,8,64]{0,3,2,1:T(8,128)(2,1)S(1)} %copy.46, bf16[3,3,64,64]{3,2,1,0:T(8,128)(2,1)S(1)} %bitcast.44), kind=kOutput, calls=%fused_computation.5 | convolution fusion | flops 256114688 | bytes 2170880 | tf_op jit(solution)/shard_map/conv_general_dilated | solution.py:46
  30.0 0.0 copy-done
  30.0 0.0 copy-start.6
  30.0 0.0 copy-start.7
  30.0 0.7 copy.42
  30.7 0.6 reshape.68
  31.3 0.0 copy-done.6
  31.3 0.0 copy-done.7
  31.3 0.2 convert_reduce_fusion
  31.5 0.6 convolution_convert_fusion
  32.1 0.1 broadcast_in_dim.8
  32.2 0.1 mul.60
  32.3 0.6 copy.44
  32.9 21.1 %all-to-all-done = bf16[64,2,8,512]{3,2,1,0:T(8,128)(2,1)S(1)} async-done(((bf16[64,2,8,512]{3,2,1,0:T(8,128)(2,1)}), bf16[64,2,8,512]{3,2,1,0:T(8,128)(2,1)S(1)}, u32[]{:S(2)}, u32[]{:S(2)}) %all-to-all-start) | async-done | bytes 1048608 | tf_op jit(solution)/shard_map/all_to_all | solution.py:94
  54.0 1.4 gather_fusion
  55.4 1.5 %reshape.74 = f32[64,8,8,64]{3,2,1,0:T(8,128)S(1)} reshape(bf16[32,2,8,512]{3,2,1,0:T(8,128)(2,1)} %gather_fusion) | data formatting | bytes 1572864 | tf_op jit(solution)/shard_map/convert_element_type | solution.py:110
  56.9 0.0 copy-start.1
  56.9 2.9 %fusion.1 = bf16[64,8,8,64]{3,0,2,1:T(8,128)(2,1)S(1)} fusion(f32[64,8,8,64]{3,0,2,1:T(8,128)} %get-tuple-element.6, f32[64,8,8,64]{3,2,1,0:T(8,128)S(1)} %reshape.74, f32[64]{0:T(128)S(1)} %mul.60), kind=kLoop, calls=%fused_computation.3 | loop fusion | flops 786432 | bytes 2621696 | tf_op jit(solution)/shard_map/convert_element_type | solution.py:112
  59.9 0.0 copy-start.2
  59.9 1.0 copy-done.2
  60.9 0.0 copy-done.1
  60.9 1.4 fusion.14
  62.3 0.1 reshape_reshape.4
  62.5 0.1 copy.52
  62.6 0.1 pad_maximum_fusion
  62.7 45.8 %all_to_all.22 = bf16[32,5,8,512]{3,2,1,0:T(8,128)(2,1)S(1)} all-to-all(bf16[32,5,8,512]{3,2,1,0:T(8,128)(2,1)S(1)} %pad_maximum_fusion), channel_id=1, replica_groups=mesh['grp'=32,'slab'=32] {'slab'}, dimensions={0} | all-to-all | bytes 2621440 | tf_op jit(solution)/shard_map/all_to_all | solution.py:129
  108.5 0.0 copy-start.3
  108.6 0.1 copy.53
  108.7 0.1 broadcast_in_dim.9
  108.8 20.0 %all_to_all.23 = f32[32,1,1152]{2,1,0:T(1,128)S(1)} all-to-all(f32[32,1,1152]{2,1,0:T(1,128)S(1)} %broadcast_in_dim.9), channel_id=1, replica_groups=mesh['grp'=32,'slab'=32] {'grp'}, dimensions={0} | all-to-all | bytes 294912 | tf_op jit(solution)/shard_map/all_to_all | solution.py:27
  128.8 0.1 reduce_sum.42
  128.9 0.7 broadcast_in_dim.10
  129.7 7.0 %all-to-all-start.3 = ((f32[32,1,1152]{2,1,0:T(1,128)}), f32[32,1,1152]{2,1,0:T(1,128)S(1)}, u32[]{:S(2)}, u32[]{:S(2)}) async-start(f32[32,1,1152]{2,1,0:T(1,128)} %broadcast_in_dim.10), calls=%async_computation.3 | async-start | bytes 294912 | tf_op jit(solution)/shard_map/all_to_all | solution.py:27
  136.7 0.0 copy-done.3
  136.7 2.6 %multiply_convert_fusion = bf16[64,8,8,64]{3,0,2,1:T(8,128)(2,1)S(1)} fusion(bf16[64,8,8,64]{3,0,2,1:T(8,128)(2,1)S(1)} %copy-done.3, bf16[3,3,64,64]{3,2,1,0:T(8,128)(2,1)S(1)} %bitcast.45, f32[64]{0:T(128)S(1)} %mul.60), kind=kOutput, calls=%fused_computation.4 | convolution fusion | flops 254279680 | bytes 1122560 | tf_op jit(solution)/shard_map/conv_general_dilated | solution.py:58
  139.3 0.7 copy.47
  139.9 1.4 reshape.72
  141.4 1.1 slice.22
  142.5 6.7 %all-to-all-done.3 = f32[32,1,1152]{2,1,0:T(1,128)S(1)} async-done(((f32[32,1,1152]{2,1,0:T(1,128)}), f32[32,1,1152]{2,1,0:T(1,128)S(1)}, u32[]{:S(2)}, u32[]{:S(2)}) %all-to-all-start.3) | async-done | bytes 147488 | tf_op jit(solution)/shard_map/all_to_all | solution.py:27
  149.2 0.4 multiply_reduce_fusion
  149.6 0.1 mul.66
  149.7 0.8 copy.49
  (11 shorter events, 0.1 us)
Async XLA Ops:
  0.6 23.4 %copy-start.4 = (bf16[32,2,8,512]{3,2,1,0:T(8,128)(2,1)S(1)}, bf16[32,2,8,512]{3,2,1,0:T(8,128)(2,1)}, u32[]{:S(2)}) copy-start(bf16[32,2,8,512]{3,2,1,0:T(8,128)(2,1)} %param.5) | copy-start | bytes 1572868
  0.6 53.4 %all-to-all-start = ((bf16[64,2,8,512]{3,2,1,0:T(8,128)(2,1)}), bf16[64,2,8,512]{3,2,1,0:T(8,128)(2,1)S(1)}, u32[]{:S(2)}, u32[]{:S(2)}) async-start(bf16[64,2,8,512]{3,2,1,0:T(8,128)(2,1)} %param.9), calls=%async_computation | async-start | bytes 2097152 | tf_op jit(solution)/shard_map/all_to_all | solution.py:94
  24.1 1.8 %copy-start.5 = (bf16[576,64]{0,1:T(8,128)(2,1)S(1)}, bf16[576,64]{0,1:T(8,128)(2,1)}, u32[]{:S(2)}) copy-start(bf16[576,64]{0,1:T(8,128)(2,1)} %param.6) | copy-start | bytes 221188
  25.9 4.1 %copy-start = (bf16[64,8,8,64]{0,3,2,1:T(8,128)(2,1)}, bf16[64,8,8,64]{0,3,2,1:T(8,128)(2,1)S(1)}, u32[]{:S(2)}) copy-start(bf16[64,8,8,64]{0,3,2,1:T(8,128)(2,1)S(1)} %copy.46) | copy-start | bytes 1572868
  30.0 1.3 copy-start.6
  30.0 1.3 copy-start.7
  56.9 3.9 %copy-start.1 = (bf16[64,8,8,64]{0,3,2,1:T(8,128)(2,1)S(1)}, bf16[64,8,8,64]{0,3,2,1:T(8,128)(2,1)}, u32[]{:S(2)}) copy-start(bf16[64,8,8,64]{0,3,2,1:T(8,128)(2,1)} %copy-done) | copy-start | bytes 1572868
  59.9 1.0 copy-start.2
  108.5 28.1 %copy-start.3 = (bf16[64,8,8,64]{3,0,2,1:T(8,128)(2,1)S(1)}, bf16[64,8,8,64]{3,0,2,1:T(8,128)(2,1)}, u32[]{:S(2)}) copy-start(bf16[64,8,8,64]{3,0,2,1:T(8,128)(2,1)} %copy-done.2) | copy-start | bytes 1572868
  129.7 19.5 %all-to-all-start.3 = ((f32[32,1,1152]{2,1,0:T(1,128)}), f32[32,1,1152]{2,1,0:T(1,128)S(1)}, u32[]{:S(2)}, u32[]{:S(2)}) async-start(f32[32,1,1152]{2,1,0:T(1,128)} %broadcast_in_dim.10), calls=%async_computation.3 | async-start | bytes 294912 | tf_op jit(solution)/shard_map/all_to_all | solution.py:27

commit v5 on v4

--- a/solution.py
+++ b/solution.py
@@ -90,14 +90,24 @@
     placer = (
         (jnp.arange(slot_count)[:, None] == slot_ids[None, :]) & (occupancy[None, :] == 1)
     ).astype(jnp.bfloat16)
-    kernel = conv_weight.reshape(3, 3, C, C)
     upstream_slots = lax.all_to_all(cotangent, "slab", split_axis=0, concat_axis=0, tiled=True)
 
     count = per_owner
-    planes = tiles.reshape(count * TD, TH, TW, C)
-    pre = conv_forward(planes, kernel)
+    lanes = TW * C
+    kernel = conv_weight.reshape(3, 3, C, C)
+    shifts = (jnp.arange(TW)[None, :, None] == jnp.arange(TW)[None, None, :] + jnp.arange(3)[:, None, None] - 1)
+    band = jnp.einsum(
+        "bwv,abco->awcvo", shifts.astype(jnp.bfloat16), kernel, preferred_element_type=jnp.float32
+    ).astype(jnp.bfloat16).reshape(3, lanes, lanes)
+    planes = tiles.reshape(count * TD, TH, lanes)
+    padded = jnp.pad(planes, ((0, 0), (1, 1), (0, 0)))
+    rows_at = [padded[:, a : a + TH, :].reshape(-1, lanes) for a in range(3)]
+    pre = sum(
+        jnp.dot(rows_at[a], band[a], preferred_element_type=jnp.float32) for a in range(3)
+    )
+
     sig = jax.nn.sigmoid(pre)
-    act_tiles = (pre * sig).astype(jnp.bfloat16).reshape(count, TD, TH, TW * C)
+    act_tiles = (pre * sig).astype(jnp.bfloat16).reshape(count, TD, TH, lanes)
     slope = sig * (1.0 + pre * (1.0 - sig))
     outgoing = jnp.einsum(
         "sk,kdhx->sdhx", placer, act_tiles, preferred_element_type=jnp.float32
@@ -105,15 +115,28 @@
     outgoing, slope = lax.optimization_barrier((outgoing, slope))
 
     upstream = jnp.take(upstream_slots, slot_ids, axis=0, mode="clip")
-    mask = occupancy.astype(jnp.float32)
-    plane_mask = jnp.repeat(mask, TD)
-    grad_pre = upstream.reshape(count * TD, TH, TW, C).astype(jnp.float32) * slope
-    grad_pre = grad_pre * plane_mask[:, None, None, None]
-    grad_pre = grad_pre.astype(jnp.bfloat16)
-    back = conv_input_grad(grad_pre, kernel)
-    wgrad = conv_kernel_grad(planes, grad_pre).reshape(9 * C, C)
-    back = back * plane_mask[:, None, None, None]
-    input_grad = back.astype(jnp.bfloat16).reshape(count, TD, TH, TW * C)
+    row_mask = jnp.repeat(occupancy.astype(jnp.float32), TD * TH)[:, None]
+    grad_pre = (upstream.reshape(-1, lanes).astype(jnp.float32) * slope * row_mask).astype(jnp.bfloat16)
+
+    picks = shifts.astype(jnp.float32)[:, :, None, :, None]
+    pieces = []
+    for a in range(3):
+        block = jnp.dot(rows_at[a].T, grad_pre, preferred_element_type=jnp.float32)
+        block = block.reshape(1, TW, C, TW, C)
+        pieces.append(jnp.sum(block * picks, axis=(1, 3)))
+    wgrad = jnp.stack(pieces).reshape(9 * C, C)
+
+    grad_planes = jnp.pad(grad_pre.reshape(count * TD, TH, lanes), ((0, 0), (1, 1), (0, 0)))
+    back = sum(
+        lax.dot_general(
+            grad_planes[:, 2 - a : 2 - a + TH, :].reshape(-1, lanes),
+            band[a],
+            (((1,), (1,)), ((), ())),
+            preferred_element_type=jnp.float32,
+        )
+        for a in range(3)
+    )
+    input_grad = (back * row_mask).astype(jnp.bfloat16).reshape(count, TD, TH, lanes)
 
     flat_w = wgrad.reshape(n_slab, -1)
     high = lax.reduce_precision(flat_w, exponent_bits=8, mantissa_bits=7)

time: 151 us -> 161 us (1.066)
  blocking collectives: 65.8 us -> 45.8 us
  starting transfers between devices: 30.4 us -> 40.7 us
  local copies, waits for them, and re-layouts: 13.1 us -> 22.8 us
  waiting for transfers between devices: 27.8 us -> 33.5 us
  matrix products: 8.55 us -> 12 us
    all_to_all x1 -> x0, blocking collectives: 20 us -> none  [sent_to_all(): lax.all_to_all(jnp.broadcast_to(x[None], (size, *x.shape)), axis, 0, 0, t...]
    dot_general x0 -> x10, matrix products: none -> 11.4 us  [the longest x3 4.41 us: local(): lax.dot_general(grad_planes[:, 2 - a:2 - a + TH, :].reshape(-1, lanes), b...]
    all_to_all x1 -> x2, waiting for transfers between devices: 6.71 us -> 17 us  [sent_to_all(): lax.all_to_all(jnp.broadcast_to(x[None], (size, *x.shape)), axis, 0, 0, t...]
    all_to_all x1 -> x2, starting transfers between devices: 6.98 us -> 17.2 us  [sent_to_all(): lax.all_to_all(jnp.broadcast_to(x[None], (size, *x.shape)), axis, 0, 0, t...]
    conv_general_dilated x3 -> x0, matrix products: 7.99 us -> none  [the longest x1 3.97 us: conv_forward(): lax.conv_general_dilated(planes, kernel, (1, 1), ((1, 1), (1, 1)), dimens...]
    dot_general x0 -> x6, local copies, waits for them, and re-layouts: none -> 5.63 us  [local(): block = jnp.dot(rows_at[a].T, grad_pre, preferred_element_type=jnp.float32)]
    all_to_all x1, waiting for transfers between devices: 21.1 us -> 16.5 us  [local(): lax.all_to_all(cotangent, 'slab', split_axis=0, concat_axis=0, tiled=True)]
    mul x1 -> x3, local copies, waits for them, and re-layouts: 0.11 us -> 4.22 us  [the longest x2 4.14 us: local(): pieces.append(jnp.sum(block * picks, axis=(1, 3)))]
  transfers between devices with their start and end apart: 2 -> 3, of which waited for: 2 -> 3; matrix products, arithmetic and copies ran while one was open for 10% -> 12% of each run, Pallas kernels for 0% -> 0%
where the time goes in v5:
time: 161 us; the launch traced here: 160 us
  blocking collectives  45.8 us (28%)
  starting transfers between devices  40.7 us (25%)
  waiting for transfers between devices  33.5 us (21%)
  local copies, waits for them, and re-layouts  22.8 us (14%)
  matrix products  12 us (7%)
  other arithmetic  4.28 us (3%)
    all_to_all x1, blocking collectives, local(): lax.all_to_all(payload, 'slab', split_axis=0, concat_axis=0, tiled=True)  45.8 us
    all_to_all x1, starting transfers between devices, local(): lax.all_to_all(cotangent, 'slab', split_axis=0, concat_axis=0, tiled=True)  23.5 us
    all_to_all x2, starting transfers between devices, sent_to_all(): lax.all_to_all(jnp.broadcast_to(x[None], (size, *x.shape)), axis, 0, 0, t...  17.2 us
    all_to_all x2, waiting for transfers between devices, sent_to_all(): lax.all_to_all(jnp.broadcast_to(x[None], (size, *x.shape)), axis, 0, 0, t...  17 us
    all_to_all x1, waiting for transfers between devices, local(): lax.all_to_all(cotangent, 'slab', split_axis=0, concat_axis=0, tiled=True)  16.5 us
    dot_general x6, local copies, waits for them, and re-layouts, local(): block = jnp.dot(rows_at[a].T, grad_pre, preferred_element_type=jnp.float32)  5.63 us
    dot_general x3, matrix products, local(): lax.dot_general(grad_planes[:, 2 - a:2 - a + TH, :].reshape(-1, lanes), b...  4.41 us
    mul x2, local copies, waits for them, and re-layouts, local(): pieces.append(jnp.sum(block * picks, axis=(1, 3)))  4.14 us
  transfers between devices with their start and end apart: 3, of which 3 were waited for; matrix products, arithmetic and copies ran while one was open for 12% of the time, Pallas kernels for 0%

profile of v5, /device:TPU:1, one launch (start us, length us, event | category | flops | bytes accessed | tf_op | source)
XLA Modules:
  0.0 160.1 jit_solution(2299067214661746707)
XLA Ops:
  0.6 0.0 copy-start.12
  0.6 0.0 copy-start.9
  0.7 0.0 copy-start
  0.7 23.5 %all-to-all-start = ((bf16[64,2,8,512]{3,2,1,0:T(8,128)(2,1)}), bf16[64,2,8,512]{3,2,1,0:T(8,128)(2,1)}, u32[]{:S(2)}, u32[]{:S(2)}) async-start(bf16[64,2,8,512]{3,2,1,0:T(8,128)(2,1)} %param.9), calls=%async_computation | async-start | bytes 2097152 | tf_op jit(solution)/shard_map/all_to_all | solution.py:93
  24.1 0.0 copy-done.12
  24.2 0.1 broadcast_in_dim.7
  24.2 0.1 mul.101
  24.3 0.0 copy-done.9
  24.4 0.1 copy.54
  24.5 0.0 copy-done
  24.5 0.2 fusion.19
  24.7 1.0 copy.63
  25.7 1.0 copy.58
  26.7 1.3 convert_bitcast_fusion
  28.1 1.2 fusion.39
  29.3 0.6 squeeze.17
  29.9 0.0 copy-start.5
  29.9 2.1 %squeeze.18 = bf16[512,512]{1,0:T(8,128)(2,1)S(1)} reshape(bf16[1,8,64,8,64]{4,3,2,0,1:T(8,128)(2,1)} %get-tuple-element.25) | data formatting | bytes 1048576 | tf_op jit(solution)/shard_map/squeeze | solution.py:106
  32.0 0.6 squeeze.16
  32.6 0.0 copy-start.1
  32.6 0.0 copy-done.13
  32.6 0.2 convert_reduce_fusion
  32.8 0.4 fusion.15
  33.3 0.4 fusion.13
  33.7 1.7 %add_multiply_fusion = (f32[512,512]{1,0:T(8,128)}, bf16[512,512]{1,0:T(8,128)(2,1)S(1)}) fusion(f32[512,512]{1,0:T(8,128)S(1)} %fusion.13, f32[512,512]{1,0:T(8,128)S(1)} %fusion.15, bf16[512,512]{1,0:T(8,128)(2,1)S(1)} %bitcast.119, bf16[512,512]{1,0:T(8,128)(2,1)S(1)} %squeeze.17), kind=kOutput, calls=%fused_computation.22 | convolution fusion | flops 271319040 | bytes 4718592 | tf_op jit(solution)/shard_map/dot_general | solution.py:106
  35.5 0.6 convolution_convert_fusion
  36.0 1.6 copy.57
  37.6 16.5 %all-to-all-done = bf16[64,2,8,512]{3,2,1,0:T(8,128)(2,1)} async-done(((bf16[64,2,8,512]{3,2,1,0:T(8,128)(2,1)}), bf16[64,2,8,512]{3,2,1,0:T(8,128)(2,1)}, u32[]{:S(2)}, u32[]{:S(2)}) %all-to-all-start) | async-done | bytes 1048608 | tf_op jit(solution)/shard_map/all_to_all | solution.py:93
  54.1 1.8 %gather_fusion = bf16[32,2,8,512]{3,2,1,0:T(8,128)(2,1)S(1)} fusion(bf16[64,2,8,512]{3,2,1,0:T(8,128)(2,1)} %all-to-all-done, s32[1024]{0:T(1024)S(1)} %pad_clamp_fusion), kind=kCustom, calls=%fused_computation | custom fusion | bytes 1048704 | tf_op jit(solution)/shard_map/jit(_take)/gather | solution.py:117
  56.0 0.0 copy-done.10
  56.0 0.0 copy-done.8
  56.0 0.2 fusion.5
  56.1 0.5 convolution_bitcast_fusion.1
  56.6 1.0 copy.59
  57.6 1.8 %mul.107 = f32[8,64,8,64]{1,0,3,2:T(8,128)} reshape(f32[512,512]{0,1:T(8,128)S(1)} %convolution_bitcast_fusion.1) | data formatting | bytes 2097152 | tf_op jit(solution)/shard_map/mul | solution.py:126
  59.4 2.4 %copy.62 = f32[8,64,8,64]{3,2,1,0:T(8,128)S(1)} copy(f32[8,64,8,64]{1,0,3,2:T(8,128)} %mul.107) | data formatting | bytes 2097152 | tf_op jit(solution)/shard_map/mul | solution.py:126
  61.8 1.9 %fusion.41 = f32[8,64,8,64]{3,1,2,0:T(8,128)S(1)} fusion(bf16[8,64,512,1]{2,1,3,0:T(8,128)(2,1)} %bitcast.125, bf16[8,64,512,1]{2,1,0,3:T(8,128)(2,1)} %bitcast.121), kind=kOutput, calls=%fused_computation.73 | convolution fusion | flops 268435456 | bytes 2097152 | tf_op jit(solution)/shard_map/dot_general | solution.py:124
  63.7 0.0 copy-start.3
  63.7 0.0 copy-start.7
  63.7 1.2 copy.64
  64.9 0.7 fusion.40
  65.7 1.2 copy.60
  66.9 3.2 %multiply_reduce_fusion.2 = (f32[3,64,64]{2,1,0:T(8,128)S(1)}, f32[3,64,64]{2,1,0:T(8,128)S(1)}, f32[3,64,64]{2,1,0:T(8,128)S(1)}) fusion(f32[3,8,8]{2,1,0:T(8,128)S(1)} %copy.61, f32[8,64,8,64]{3,2,1,0:T(8,128)S(1)} %copy.60, f32[8,64,8,64]{3,2,1,0:T(8,128)S(1)} %copy.62, f32[8,64,8,64]{3,2,1,0:T(8,128)S(1)} %copy.64), kind=kLoop, calls=%fused_computation.3 | loop fusion | flops 4681728 | bytes 3293952 | tf_op jit(solution)/shard_map/reduce_sum | solution.py:126
  70.1 0.1 reshape_reshape.4
  70.2 0.1 copy.72
  70.3 0.9 copy-done.4
  71.2 0.1 pad_maximum_fusion
  71.4 45.8 %all_to_all.22 = bf16[32,5,8,512]{3,2,1,0:T(8,128)(2,1)S(1)} all-to-all(bf16[32,5,8,512]{3,2,1,0:T(8,128)(2,1)S(1)} %pad_maximum_fusion), channel_id=1, replica_groups=mesh['grp'=32,'slab'=32] {'slab'}, dimensions={0} | all-to-all | bytes 2621440 | tf_op jit(solution)/shard_map/all_to_all | solution.py:152
  117.2 0.1 copy.73
  117.3 0.0 copy-start.6
  117.4 0.7 broadcast_in_dim.8
  118.2 10.3 %all-to-all-start.2 = ((f32[32,1,1152]{2,1,0:T(1,128)}), f32[32,1,1152]{2,1,0:T(1,128)S(1)}, u32[]{:S(2)}, u32[]{:S(2)}) async-start(f32[32,1,1152]{2,1,0:T(1,128)} %broadcast_in_dim.8), calls=%async_computation.2 | async-start | bytes 294912 | tf_op jit(solution)/shard_map/all_to_all | solution.py:27
  128.4 1.4 fusion.7
  129.9 8.5 %all-to-all-done.2 = f32[32,1,1152]{2,1,0:T(1,128)S(1)} async-done(((f32[32,1,1152]{2,1,0:T(1,128)}), f32[32,1,1152]{2,1,0:T(1,128)S(1)}, u32[]{:S(2)}, u32[]{:S(2)}) %all-to-all-start.2) | async-done | bytes 147488 | tf_op jit(solution)/shard_map/all_to_all | solution.py:27
  138.4 0.1 reduce_sum.72
  138.5 0.7 broadcast_in_dim.10
  139.2 7.0 %all-to-all-start.3 = ((f32[32,1,1152]{2,1,0:T(1,128)}), f32[32,1,1152]{2,1,0:T(1,128)S(1)}, u32[]{:S(2)}, u32[]{:S(2)}) async-start(f32[32,1,1152]{2,1,0:T(1,128)} %broadcast_in_dim.10), calls=%async_computation.3 | async-start | bytes 294912 | tf_op jit(solution)/shard_map/all_to_all | solution.py:27
  146.2 1.7 %convolution_add_fusion.1 = f32[512,512]{1,0:T(8,128)S(1)} fusion(f32[512,512]{1,0:T(8,128)} %fusion.7, bf16[512,512]{1,0:T(8,128)(2,1)S(1)} %fusion.5, bf16[512,512]{1,0:T(8,128)(2,1)S(1)} %copy-done.6), kind=kOutput, calls=%fused_computation.11 | convolution fusion | flops 268697600 | bytes 3145728 | tf_op jit(solution)/shard_map/dot_general | solution.py:131
  147.9 1.3 fusion.3
  149.2 1.1 slice.61
  150.3 8.4 %all-to-all-done.3 = f32[32,1,1152]{2,1,0:T(1,128)S(1)} async-done(((f32[32,1,1152]{2,1,0:T(1,128)}), f32[32,1,1152]{2,1,0:T(1,128)S(1)}, u32[]{:S(2)}, u32[]{:S(2)}) %all-to-all-start.3) | async-done | bytes 147488 | tf_op jit(solution)/shard_map/all_to_all | solution.py:27
  158.7 0.4 multiply_reduce_fusion.3
  159.1 0.1 mul.115
  159.3 0.8 copy.66
  (28 shorter events, 0.2 us)
Async XLA Ops:
  0.6 23.5 %copy-start.12 = (s32[32]{0:T(128)S(1)}, s32[32]{0:T(128)}, u32[]{:S(2)}) copy-start(s32[32]{0:T(128)} %param.8) | copy-start | bytes 388
  0.6 23.7 %copy-start.9 = (bf16[576,64]{0,1:T(8,128)(2,1)S(1)}, bf16[576,64]{0,1:T(8,128)(2,1)}, u32[]{:S(2)}) copy-start(bf16[576,64]{0,1:T(8,128)(2,1)} %param.6) | copy-start | bytes 221188
  0.7 23.8 %copy-start = (bf16[32,2,8,512]{3,2,1,0:T(8,128)(2,1)S(1)}, bf16[32,2,8,512]{3,2,1,0:T(8,128)(2,1)}, u32[]{:S(2)}) copy-start(bf16[32,2,8,512]{3,2,1,0:T(8,128)(2,1)} %param.5) | copy-start | bytes 1572868
  0.7 53.5 %all-to-all-start = ((bf16[64,2,8,512]{3,2,1,0:T(8,128)(2,1)}), bf16[64,2,8,512]{3,2,1,0:T(8,128)(2,1)}, u32[]{:S(2)}, u32[]{:S(2)}) async-start(bf16[64,2,8,512]{3,2,1,0:T(8,128)(2,1)} %param.9), calls=%async_computation | async-start | bytes 2097152 | tf_op jit(solution)/shard_map/all_to_all | solution.py:93
  24.3 31.6 %copy-start.10 = (f32[512]{0:T(512)}, f32[512]{0:T(512)S(1)}, u32[]{:S(2)}) copy-start(f32[512]{0:T(512)S(1)} %mul.101) | copy-start | bytes 6148
  29.3 3.3 %copy-start.13 = (s32[32,1]{0,1:T(1,128)S(1)}, s32[32,1]{0,1:T(1,128)}, u32[]{:S(2)}) copy-start(s32[32,1]{0,1:T(1,128)} %param.7) | copy-start | bytes 388
  29.9 3.8 %copy-start.5 = (bf16[512,512]{1,0:T(8,128)(2,1)}, bf16[512,512]{1,0:T(8,128)(2,1)S(1)}, u32[]{:S(2)}) copy-start(bf16[512,512]{1,0:T(8,128)(2,1)S(1)} %squeeze.17) | copy-start | bytes 1572868
  32.6 1.1 copy-start.1
  35.5 20.5 %copy-start.8 = (f32[512,512]{1,0:T(8,128)S(1)}, f32[512,512]{1,0:T(8,128)}, u32[]{:S(2)}) copy-start(f32[512,512]{1,0:T(8,128)} %get-tuple-element.6) | copy-start | bytes 3145732
  63.7 1.2 copy-start.3
  63.7 1.2 copy-start.7
  70.0 1.2 copy-start.4
  71.4 57.0 %copy-start.2 = (bf16[512,512]{1,0:T(8,128)(2,1)S(1)}, bf16[512,512]{1,0:T(8,128)(2,1)}, u32[]{:S(2)}) copy-start(bf16[512,512]{1,0:T(8,128)(2,1)} %copy-done.1) | copy-start | bytes 1572868
  117.3 28.9 %copy-start.6 = (bf16[512,512]{1,0:T(8,128)(2,1)S(1)}, bf16[512,512]{1,0:T(8,128)(2,1)}, u32[]{:S(2)}) copy-start(bf16[512,512]{1,0:T(8,128)(2,1)} %copy-done.5) | copy-start | bytes 1572868
  118.2 20.2 %all-to-all-start.2 = ((f32[32,1,1152]{2,1,0:T(1,128)}), f32[32,1,1152]{2,1,0:T(1,128)S(1)}, u32[]{:S(2)}, u32[]{:S(2)}) async-start(f32[32,1,1152]{2,1,0:T(1,128)} %broadcast_in_dim.8), calls=%async_computation.2 | async-start | bytes 294912 | tf_op jit(solution)/shard_map/all_to_all | solution.py:27
  129.9 18.1 %copy-start.11 = (f32[512]{0:T(512)S(1)}, f32[512]{0:T(512)}, u32[]{:S(2)}) copy-start(f32[512]{0:T(512)} %copy-done.10) | copy-start | bytes 6148
  139.2 19.5 %all-to-all-start.3 = ((f32[32,1,1152]{2,1,0:T(1,128)}), f32[32,1,1152]{2,1,0:T(1,128)S(1)}, u32[]{:S(2)}, u32[]{:S(2)}) async-start(f32[32,1,1152]{2,1,0:T(1,128)} %broadcast_in_dim.10), calls=%async_computation.3 | async-start | bytes 294912 | tf_op jit(solution)/shard_map/all_to_all | solution.py:27

commit v6 on v4

--- a/solution.py
+++ b/solution.py
@@ -102,14 +102,15 @@
     outgoing = jnp.einsum(
         "sk,kdhx->sdhx", placer, act_tiles, preferred_element_type=jnp.float32
     ).astype(jnp.bfloat16)
+    slope = slope.reshape(count, TD, TH, TW * C)
     outgoing, slope = lax.optimization_barrier((outgoing, slope))
 
     upstream = jnp.take(upstream_slots, slot_ids, axis=0, mode="clip")
     mask = occupancy.astype(jnp.float32)
     plane_mask = jnp.repeat(mask, TD)
-    grad_pre = upstream.reshape(count * TD, TH, TW, C).astype(jnp.float32) * slope
-    grad_pre = grad_pre * plane_mask[:, None, None, None]
-    grad_pre = grad_pre.astype(jnp.bfloat16)
+    grad_pre = upstream.astype(jnp.float32) * slope
+    grad_pre = grad_pre * mask[:, None, None, None]
+    grad_pre = grad_pre.astype(jnp.bfloat16).reshape(count * TD, TH, TW, C)
     back = conv_input_grad(grad_pre, kernel)
     wgrad = conv_kernel_grad(planes, grad_pre).reshape(9 * C, C)
     back = back * plane_mask[:, None, None, None]

time: 151 us -> 148 us (0.980)
  waiting for transfers between devices: 27.8 us -> 22.5 us
  other arithmetic: 3.86 us -> 1.08 us
  local copies, waits for them, and re-layouts: 13.1 us -> 15.8 us
  matrix products: 8.55 us -> 11.1 us
    all_to_all x1, waiting for transfers between devices: 21.1 us -> 16.1 us  [local(): lax.all_to_all(cotangent, 'slab', split_axis=0, concat_axis=0, tiled=True)]
    mul x1 -> x2, local copies, waits for them, and re-layouts: 0.11 us -> 2.91 us  [the longest x1 2.81 us: local(): slope = sig * (1.0 + pre * (1.0 - sig))]
    convert_element_type x1, other arithmetic: 2.94 us -> 0.16 us  [local(): grad_pre = grad_pre.astype(jnp.bfloat16).reshape(count * TD, TH, TW, C)]
    convert_element_type x1 -> x0, local copies, waits for them, and re-layouts: 1.53 us -> none  [local(): upstream.reshape(count * TD, TH, TW, C).astype(jnp.float32) * slope]
  transfers between devices with their start and end apart: 2 -> 2, of which waited for: 2 -> 2; matrix products, arithmetic and copies ran while one was open for 10% -> 13% of each run, Pallas kernels for 0% -> 0%
where the time goes in v6:
time: 148 us
  blocking collectives  65.7 us (44%)
  starting transfers between devices  30.4 us (21%)
  waiting for transfers between devices  22.5 us (15%)
  local copies, waits for them, and re-layouts  15.8 us (11%)
  matrix products  11.1 us (8%)
    all_to_all x1, blocking collectives, local(): lax.all_to_all(payload, 'slab', split_axis=0, concat_axis=0, tiled=True)  45.8 us
    all_to_all x1, starting transfers between devices, local(): lax.all_to_all(cotangent, 'slab', split_axis=0, concat_axis=0, tiled=True)  23.5 us
    all_to_all x1, blocking collectives, sent_to_all(): lax.all_to_all(jnp.broadcast_to(x[None], (size, *x.shape)), axis, 0, 0, t...  19.9 us
    all_to_all x1, waiting for transfers between devices, local(): lax.all_to_all(cotangent, 'slab', split_axis=0, concat_axis=0, tiled=True)  16.1 us
    all_to_all x1, starting transfers between devices, sent_to_all(): lax.all_to_all(jnp.broadcast_to(x[None], (size, *x.shape)), axis, 0, 0, t...  6.96 us
    all_to_all x1, waiting for transfers between devices, sent_to_all(): lax.all_to_all(jnp.broadcast_to(x[None], (size, *x.shape)), axis, 0, 0, t...  6.39 us
    conv_general_dilated x1, matrix products, conv_forward(): lax.conv_general_dilated(planes, kernel, (1, 1), ((1, 1), (1, 1)), dimens...  3.98 us
  transfers between devices with their start and end apart: 2, of which 2 were waited for; matrix products, arithmetic and copies ran while one was open for 13% of the time, Pallas kernels for 0%

profile of v6, /device:TPU:1, one launch (start us, length us, event | category | flops | bytes accessed | tf_op | source)
XLA Modules:
  0.0 147.5 jit_solution(11746646309161184162)
XLA Ops:
  0.6 0.0 copy-start.1
  0.6 23.5 %all-to-all-start = ((bf16[64,2,8,512]{3,2,1,0:T(8,128)(2,1)}), bf16[64,2,8,512]{3,2,1,0:T(8,128)(2,1)}, u32[]{:S(2)}, u32[]{:S(2)}) async-start(bf16[64,2,8,512]{3,2,1,0:T(8,128)(2,1)} %param.9), calls=%async_computation | async-start | bytes 2097152 | tf_op jit(solution)/shard_map/all_to_all | solution.py:94
  24.1 0.0 copy-done.1
  24.1 0.0 copy-start.2
  24.1 0.5 reshape.70
  24.7 1.2 copy.54
  25.9 0.0 copy-done.2
  25.9 0.0 copy-start
  25.9 0.1 copy.48
  26.1 4.0 %add_multiply_fusion = (f32[64,8,8,64]{3,0,2,1:T(8,128)}, bf16[64,8,8,64]{3,0,2,1:T(8,128)(2,1)S(1)}) fusion(bf16[64,8,8,64]{0,3,2,1:T(8,128)(2,1)S(1)} %copy.54, bf16[3,3,64,64]{3,2,1,0:T(8,128)(2,1)S(1)} %bitcast.44), kind=kOutput, calls=%fused_computation.2 | convolution fusion | flops 256114688 | bytes 2170880 | tf_op jit(solution)/shard_map/conv_general_dilated | solution.py:46
  30.0 0.0 copy-done
  30.0 0.7 copy.50
  30.7 1.4 reshape.72
  32.1 2.8 %copy.52 = f32[64,8,8,64]{3,2,1,0:T(8,128)S(1)} copy(f32[64,8,8,64]{3,0,2,1:T(8,128)} %get-tuple-element.21) | data formatting | bytes 2097152 | tf_op jit(solution)/shard_map/mul | solution.py:101
  34.9 0.0 copy-start.3
  35.0 0.0 copy-start.4
  35.0 0.5 reshape.73
  35.5 0.1 copy-done.3
  35.6 0.0 copy-done.4
  35.6 0.2 convert_reduce_fusion
  35.8 1.6 %convolution_convert_fusion = bf16[64,2,8,512]{3,0,2,1:T(8,128)(2,1)S(1)} fusion(bf16[32,2,8,512]{3,2,1,0:T(8,128)(2,1)} %reshape.72, s32[32]{0:T(128)S(1)} %multiply_add_fusion, pred[32]{0:T(512)(128)(4,1)S(1)} %broadcast_compare_fusion), kind=kOutput, calls=%fused_computation.5 | convolution fusion | flops 34082816 | bytes 1573024 | tf_op jit(solution)/shard_map/sk,kdhx->sdhx/dot_general | solution.py:102
  37.4 0.6 copy.53
  38.0 16.1 %all-to-all-done = bf16[64,2,8,512]{3,2,1,0:T(8,128)(2,1)} async-done(((bf16[64,2,8,512]{3,2,1,0:T(8,128)(2,1)}), bf16[64,2,8,512]{3,2,1,0:T(8,128)(2,1)}, u32[]{:S(2)}, u32[]{:S(2)}) %all-to-all-start) | async-done | bytes 1048608 | tf_op jit(solution)/shard_map/all_to_all | solution.py:94
  54.1 1.8 %gather_fusion = bf16[32,2,8,512]{3,2,1,0:T(8,128)(2,1)S(1)} fusion(bf16[64,2,8,512]{3,2,1,0:T(8,128)(2,1)} %all-to-all-done, s32[1024]{0:T(1024)S(1)} %pad_clamp_fusion), kind=kCustom, calls=%fused_computation | custom fusion | bytes 1048704 | tf_op jit(solution)/shard_map/jit(_take)/gather | solution.py:108
  55.9 0.2 multiply_convert_fusion.2
  56.1 0.5 reshape.75
  56.6 2.8 %fusion.1 = f32[3,3,64,64]{3,2,1,0:T(8,128)S(1)} fusion(bf16[64,8,8,64]{0,3,2,1:T(8,128)(2,1)} %copy-done, bf16[64,8,8,64]{3,2,1,0:T(8,128)(2,1)S(1)} %reshape.75), kind=kOutput, calls=%fused_computation.9 | convolution fusion | flops 253755392 | bytes 1196032 | tf_op jit(solution)/shard_map/conv_general_dilated | solution.py:69
  59.4 0.1 reshape_reshape.4
  59.6 0.1 copy.62
  59.7 0.1 pad_maximum_fusion
  59.8 45.8 %all_to_all.22 = bf16[32,5,8,512]{3,2,1,0:T(8,128)(2,1)S(1)} all-to-all(bf16[32,5,8,512]{3,2,1,0:T(8,128)(2,1)S(1)} %pad_maximum_fusion), channel_id=1, replica_groups=mesh['grp'=32,'slab'=32] {'slab'}, dimensions={0} | all-to-all | bytes 2621440 | tf_op jit(solution)/shard_map/all_to_all | solution.py:130
  105.7 0.1 copy.63
  105.8 0.1 broadcast_in_dim.9
  105.9 19.9 %all_to_all.23 = f32[32,1,1152]{2,1,0:T(1,128)S(1)} all-to-all(f32[32,1,1152]{2,1,0:T(1,128)S(1)} %broadcast_in_dim.9), channel_id=1, replica_groups=mesh['grp'=32,'slab'=32] {'grp'}, dimensions={0} | all-to-all | bytes 294912 | tf_op jit(solution)/shard_map/all_to_all | solution.py:27
  125.8 0.1 reduce_sum.42
  125.9 0.7 broadcast_in_dim.10
  126.7 7.0 %all-to-all-start.3 = ((f32[32,1,1152]{2,1,0:T(1,128)}), f32[32,1,1152]{2,1,0:T(1,128)S(1)}, u32[]{:S(2)}, u32[]{:S(2)}) async-start(f32[32,1,1152]{2,1,0:T(1,128)} %broadcast_in_dim.10), calls=%async_computation.3 | async-start | bytes 294912 | tf_op jit(solution)/shard_map/all_to_all | solution.py:27
  133.6 0.1 broadcast_in_dim.8
  133.7 0.1 mul.64
  133.8 2.8 %multiply_convert_fusion = bf16[64,8,8,64]{3,0,2,1:T(8,128)(2,1)S(1)} fusion(bf16[3,3,64,64]{3,2,1,0:T(8,128)(2,1)S(1)} %bitcast.45, f32[64]{0:T(128)S(1)} %mul.64, bf16[64,8,8,64]{3,2,1,0:T(8,128)(2,1)S(1)} %reshape.75), kind=kOutput, calls=%fused_computation.1 | convolution fusion | flops 254279680 | bytes 1122560 | tf_op jit(solution)/shard_map/conv_general_dilated | solution.py:58
  136.6 0.7 copy.57
  137.3 1.4 reshape.78
  138.7 1.1 slice.22
  139.8 6.4 %all-to-all-done.3 = f32[32,1,1152]{2,1,0:T(1,128)S(1)} async-done(((f32[32,1,1152]{2,1,0:T(1,128)}), f32[32,1,1152]{2,1,0:T(1,128)S(1)}, u32[]{:S(2)}, u32[]{:S(2)}) %all-to-all-start.3) | async-done | bytes 147488 | tf_op jit(solution)/shard_map/all_to_all | solution.py:27
  146.2 0.4 multiply_reduce_fusion
  146.6 0.1 mul.69
  146.7 0.8 copy.59
  (11 shorter events, 0.1 us)
Async XLA Ops:
  0.6 23.5 %copy-start.1 = (bf16[32,2,8,512]{3,2,1,0:T(8,128)(2,1)S(1)}, bf16[32,2,8,512]{3,2,1,0:T(8,128)(2,1)}, u32[]{:S(2)}) copy-start(bf16[32,2,8,512]{3,2,1,0:T(8,128)(2,1)} %param.5) | copy-start | bytes 1572868
  0.6 53.5 %all-to-all-start = ((bf16[64,2,8,512]{3,2,1,0:T(8,128)(2,1)}), bf16[64,2,8,512]{3,2,1,0:T(8,128)(2,1)}, u32[]{:S(2)}, u32[]{:S(2)}) async-start(bf16[64,2,8,512]{3,2,1,0:T(8,128)(2,1)} %param.9), calls=%async_computation | async-start | bytes 2097152 | tf_op jit(solution)/shard_map/all_to_all | solution.py:94
  24.1 1.8 %copy-start.2 = (bf16[576,64]{0,1:T(8,128)(2,1)S(1)}, bf16[576,64]{0,1:T(8,128)(2,1)}, u32[]{:S(2)}) copy-start(bf16[576,64]{0,1:T(8,128)(2,1)} %param.6) | copy-start | bytes 221188
  25.9 4.1 %copy-start = (bf16[64,8,8,64]{0,3,2,1:T(8,128)(2,1)}, bf16[64,8,8,64]{0,3,2,1:T(8,128)(2,1)S(1)}, u32[]{:S(2)}) copy-start(bf16[64,8,8,64]{0,3,2,1:T(8,128)(2,1)S(1)} %copy.54) | copy-start | bytes 1572868
  34.9 0.7 copy-start.3
  35.0 0.7 copy-start.4
  126.7 19.5 %all-to-all-start.3 = ((f32[32,1,1152]{2,1,0:T(1,128)}), f32[32,1,1152]{2,1,0:T(1,128)S(1)}, u32[]{:S(2)}, u32[]{:S(2)}) async-start(f32[32,1,1152]{2,1,0:T(1,128)} %broadcast_in_dim.10), calls=%async_computation.3 | async-start | bytes 294912 | tf_op jit(solution)/shard_map/all_to_all | solution.py:27

commit v7 on v6

--- a/solution.py
+++ b/solution.py
@@ -105,7 +105,9 @@
     slope = slope.reshape(count, TD, TH, TW * C)
     outgoing, slope = lax.optimization_barrier((outgoing, slope))
 
-    upstream = jnp.take(upstream_slots, slot_ids, axis=0, mode="clip")
+    upstream = jnp.einsum(
+        "sk,sdhx->kdhx", placer, upstream_slots, preferred_element_type=jnp.float32
+    )
     mask = occupancy.astype(jnp.float32)
     plane_mask = jnp.repeat(mask, TD)
     grad_pre = upstream.astype(jnp.float32) * slope
@@ -131,10 +133,10 @@
     activations = arrived[:, : capacity * TD].reshape(outgoing.shape)
     got = arrived[:, capacity * TD :].reshape(n_slab, -1)[:, : 2 * share_width].astype(jnp.float32)
     share = jnp.sum(got[:, :share_width], axis=0) + jnp.sum(got[:, share_width:], axis=0)
-    share = over_copies(share, "grp")
+    scale = 1.0 / math.sqrt(per_owner * n_group * n_slab * TD * TH * TW)
+    share = over_copies(share, "grp") * scale
     summed = gathered_copies(share, "slab", 0).reshape(9 * C, C)
-    scale = 1.0 / math.sqrt(per_owner * n_group * n_slab * TD * TH * TW)
-    return (activations, input_grad, summed * scale)
+    return (activations, input_grad, summed)
 
 
 def solution(mesh):

time: 148 us -> 149 us (level)
  matrix products: 11.1 us -> 14.1 us
  local copies, waits for them, and re-layouts: 15.8 us -> 14.3 us
    dot_general x0 -> x1, matrix products: none -> 3 us  [local(): jnp.einsum('sk,sdhx->kdhx', placer, upstream_slots, preferred_element_typ...]
    gather x1 -> x0, local copies, waits for them, and re-layouts: 1.8 us -> none  [local(): upstream = jnp.take(upstream_slots, slot_ids, axis=0, mode='clip')]
where the time goes in v7:
time: 149 us
  blocking collectives  65.7 us (44%)
  starting transfers between devices  30.4 us (20%)
  waiting for transfers between devices  22.5 us (15%)
  local copies, waits for them, and re-layouts  14.3 us (10%)
  matrix products  14.1 us (9%)
    all_to_all x1, blocking collectives, local(): lax.all_to_all(payload, 'slab', split_axis=0, concat_axis=0, tiled=True)  45.9 us
    all_to_all x1, starting transfers between devices, local(): lax.all_to_all(cotangent, 'slab', split_axis=0, concat_axis=0, tiled=True)  23.5 us
    all_to_all x1, blocking collectives, sent_to_all(): lax.all_to_all(jnp.broadcast_to(x[None], (size, *x.shape)), axis, 0, 0, t...  19.9 us
    all_to_all x1, waiting for transfers between devices, local(): lax.all_to_all(cotangent, 'slab', split_axis=0, concat_axis=0, tiled=True)  16.1 us
    all_to_all x1, starting transfers between devices, sent_to_all(): lax.all_to_all(jnp.broadcast_to(x[None], (size, *x.shape)), axis, 0, 0, t...  6.96 us
    all_to_all x1, waiting for transfers between devices, sent_to_all(): lax.all_to_all(jnp.broadcast_to(x[None], (size, *x.shape)), axis, 0, 0, t...  6.39 us
    conv_general_dilated x1, matrix products, conv_forward(): lax.conv_general_dilated(planes, kernel, (1, 1), ((1, 1), (1, 1)), dimens...  3.98 us
    dot_general x1, matrix products, local(): jnp.einsum('sk,sdhx->kdhx', placer, upstream_slots, preferred_element_typ...  3 us
  transfers between devices with their start and end apart: 2, of which 2 were waited for; matrix products, arithmetic and copies ran while one was open for 13% of the time, Pallas kernels for 0%

profile of v7, /device:TPU:1, one launch (start us, length us, event | category | flops | bytes accessed | tf_op | source)
XLA Modules:
  0.0 148.8 jit_solution(11261536141139791498)
XLA Ops:
  0.6 0.0 copy-start.1
  0.6 23.5 %all-to-all-start = ((bf16[64,2,8,512]{3,2,1,0:T(8,128)(2,1)}), bf16[64,2,8,512]{3,2,1,0:T(8,128)(2,1)}, u32[]{:S(2)}, u32[]{:S(2)}) async-start(bf16[64,2,8,512]{3,2,1,0:T(8,128)(2,1)} %param.9), calls=%async_computation | async-start | bytes 2097152 | tf_op jit(solution)/shard_map/all_to_all | solution.py:94
  24.1 0.0 copy-done.1
  24.1 0.0 copy-start.2
  24.1 0.5 reshape.70
  24.7 1.2 copy.65
  25.9 0.0 copy-done.2
  25.9 0.0 copy-start
  25.9 0.1 copy.56
  26.1 4.0 %add_multiply_fusion = (f32[64,8,8,64]{3,0,2,1:T(8,128)}, bf16[64,8,8,64]{3,0,2,1:T(8,128)(2,1)S(1)}) fusion(bf16[64,8,8,64]{0,3,2,1:T(8,128)(2,1)S(1)} %copy.65, bf16[3,3,64,64]{3,2,1,0:T(8,128)(2,1)S(1)} %bitcast.39), kind=kOutput, calls=%fused_computation.1 | convolution fusion | flops 256114688 | bytes 2170880 | tf_op jit(solution)/shard_map/conv_general_dilated | solution.py:46
  30.0 0.0 copy-done
  30.0 0.7 copy.58
  30.7 1.4 reshape.72
  32.1 2.8 %copy.60 = f32[64,8,8,64]{3,2,1,0:T(8,128)S(1)} copy(f32[64,8,8,64]{3,0,2,1:T(8,128)} %get-tuple-element.21) | data formatting | bytes 2097152 | tf_op jit(solution)/shard_map/mul | solution.py:101
  34.9 0.0 copy-start.3
  35.0 0.0 copy-start.4
  35.0 0.5 reshape.73
  35.5 0.1 copy-done.3
  35.6 0.0 copy-done.4
  35.6 0.2 convert_reduce_fusion
  35.8 1.6 %convolution_convert_fusion = bf16[64,2,8,512]{3,0,2,1:T(8,128)(2,1)S(1)} fusion(bf16[32,2,8,512]{3,2,1,0:T(8,128)(2,1)} %reshape.72, s32[32]{0:T(128)S(1)} %multiply_add_fusion, pred[32]{0:T(512)(128)(4,1)S(1)} %broadcast_compare_fusion), kind=kOutput, calls=%fused_computation.4 | convolution fusion | flops 34082816 | bytes 1573024 | tf_op jit(solution)/shard_map/sk,kdhx->sdhx/dot_general | solution.py:102
  37.4 0.6 copy.61
  38.0 16.1 %all-to-all-done = bf16[64,2,8,512]{3,2,1,0:T(8,128)(2,1)} async-done(((bf16[64,2,8,512]{3,2,1,0:T(8,128)(2,1)}), bf16[64,2,8,512]{3,2,1,0:T(8,128)(2,1)}, u32[]{:S(2)}, u32[]{:S(2)}) %all-to-all-start) | async-done | bytes 1048608 | tf_op jit(solution)/shard_map/all_to_all | solution.py:94
  54.1 3.0 %fusion.1 = bf16[32,2,8,512]{3,0,2,1:T(8,128)(2,1)S(1)} fusion(f32[32,2,8,512]{3,2,1,0:T(8,128)S(1)} %reshape.73, bf16[64,2,8,512]{3,2,1,0:T(8,128)(2,1)} %all-to-all-done, f32[32]{0:T(128)S(1)} %convert_element_type.28, s32[32]{0:T(128)S(1)} %multiply_add_fusion, pred[32]{0:T(512)(128)(4,1)S(1)} %broadcast_compare_fusion), kind=kOutput, calls=%fused_computation.8 | convolution fusion | flops 34344960 | bytes 2621728 | tf_op jit(solution)/shard_map/sk,sdhx->kdhx/dot_general | solution.py:108
  57.1 0.3 copy.64
  57.4 0.5 reshape.75
  58.0 2.8 %fusion.4 = f32[3,3,64,64]{3,2,1,0:T(8,128)S(1)} fusion(bf16[64,8,8,64]{0,3,2,1:T(8,128)(2,1)} %copy-done, bf16[64,8,8,64]{3,2,1,0:T(8,128)(2,1)S(1)} %reshape.75), kind=kOutput, calls=%fused_computation.11 | convolution fusion | flops 253755392 | bytes 1196032 | tf_op jit(solution)/shard_map/conv_general_dilated | solution.py:69
  60.7 0.1 reshape_reshape.6
  60.9 0.1 copy.73
  61.0 0.1 pad_maximum_fusion
  61.1 45.9 %all_to_all.22 = bf16[32,5,8,512]{3,2,1,0:T(8,128)(2,1)S(1)} all-to-all(bf16[32,5,8,512]{3,2,1,0:T(8,128)(2,1)S(1)} %pad_maximum_fusion), channel_id=1, replica_groups=mesh['grp'=32,'slab'=32] {'slab'}, dimensions={0} | all-to-all | bytes 2621440 | tf_op jit(solution)/shard_map/all_to_all | solution.py:132
  107.0 0.1 copy.74
  107.2 0.1 broadcast_in_dim.7
  107.3 19.9 %all_to_all.23 = f32[32,1,1152]{2,1,0:T(1,128)S(1)} all-to-all(f32[32,1,1152]{2,1,0:T(1,128)S(1)} %broadcast_in_dim.7), channel_id=1, replica_groups=mesh['grp'=32,'slab'=32] {'grp'}, dimensions={0} | all-to-all | bytes 294912 | tf_op jit(solution)/shard_map/all_to_all | solution.py:27
  127.2 0.1 reduce_sum.39
  127.3 0.7 broadcast_in_dim.8
  128.0 7.0 %all-to-all-start.3 = ((f32[32,1,1152]{2,1,0:T(1,128)}), f32[32,1,1152]{2,1,0:T(1,128)S(1)}, u32[]{:S(2)}, u32[]{:S(2)}) async-start(f32[32,1,1152]{2,1,0:T(1,128)} %broadcast_in_dim.8), calls=%async_computation.3 | async-start | bytes 294912 | tf_op jit(solution)/shard_map/all_to_all | solution.py:27
  135.0 0.1 broadcast_in_dim.6
  135.1 0.1 mul.58
  135.2 2.8 %multiply_convert_fusion = bf16[64,8,8,64]{3,0,2,1:T(8,128)(2,1)S(1)} fusion(bf16[3,3,64,64]{3,2,1,0:T(8,128)(2,1)S(1)} %bitcast.40, f32[64]{0:T(128)S(1)} %mul.58, bf16[64,8,8,64]{3,2,1,0:T(8,128)(2,1)S(1)} %reshape.75), kind=kOutput, calls=%fused_computation | convolution fusion | flops 254279680 | bytes 1122560 | tf_op jit(solution)/shard_map/conv_general_dilated | solution.py:58
  137.9 0.7 copy.68
  138.6 1.4 reshape.78
  140.0 1.1 slice.20
  141.1 6.4 %all-to-all-done.3 = f32[32,1,1152]{2,1,0:T(1,128)S(1)} async-done(((f32[32,1,1152]{2,1,0:T(1,128)}), f32[32,1,1152]{2,1,0:T(1,128)S(1)}, u32[]{:S(2)}, u32[]{:S(2)}) %all-to-all-start.3) | async-done | bytes 147488 | tf_op jit(solution)/shard_map/all_to_all | solution.py:27
  147.5 0.3 reduce.1
  147.9 0.1 reshape_reshape.7
  148.0 0.8 copy.70
  (10 shorter events, 0.1 us)
Async XLA Ops:
  0.6 23.5 %copy-start.1 = (bf16[32,2,8,512]{3,2,1,0:T(8,128)(2,1)S(1)}, bf16[32,2,8,512]{3,2,1,0:T(8,128)(2,1)}, u32[]{:S(2)}) copy-start(bf16[32,2,8,512]{3,2,1,0:T(8,128)(2,1)} %param.5) | copy-start | bytes 1572868
  0.6 53.5 %all-to-all-start = ((bf16[64,2,8,512]{3,2,1,0:T(8,128)(2,1)}), bf16[64,2,8,512]{3,2,1,0:T(8,128)(2,1)}, u32[]{:S(2)}, u32[]{:S(2)}) async-start(bf16[64,2,8,512]{3,2,1,0:T(8,128)(2,1)} %param.9), calls=%async_computation | async-start | bytes 2097152 | tf_op jit(solution)/shard_map/all_to_all | solution.py:94
  24.1 1.8 %copy-start.2 = (bf16[576,64]{0,1:T(8,128)(2,1)S(1)}, bf16[576,64]{0,1:T(8,128)(2,1)}, u32[]{:S(2)}) copy-start(bf16[576,64]{0,1:T(8,128)(2,1)} %param.6) | copy-start | bytes 221188
  25.9 4.1 %copy-start = (bf16[64,8,8,64]{0,3,2,1:T(8,128)(2,1)}, bf16[64,8,8,64]{0,3,2,1:T(8,128)(2,1)S(1)}, u32[]{:S(2)}) copy-start(bf16[64,8,8,64]{0,3,2,1:T(8,128)(2,1)S(1)} %copy.65) | copy-start | bytes 1572868
  34.9 0.7 copy-start.3
  35.0 0.7 copy-start.4
  128.0 19.5 %all-to-all-start.3 = ((f32[32,1,1152]{2,1,0:T(1,128)}), f32[32,1,1152]{2,1,0:T(1,128)S(1)}, u32[]{:S(2)}, u32[]{:S(2)}) async-start(f32[32,1,1152]{2,1,0:T(1,128)} %broadcast_in_dim.8), calls=%async_computation.3 | async-start | bytes 294912 | tf_op jit(solution)/shard_map/all_to_all | solution.py:27

commit v8 on v6

--- a/solution.py
+++ b/solution.py
@@ -103,7 +103,10 @@
         "sk,kdhx->sdhx", placer, act_tiles, preferred_element_type=jnp.float32
     ).astype(jnp.bfloat16)
     slope = slope.reshape(count, TD, TH, TW * C)
-    outgoing, slope = lax.optimization_barrier((outgoing, slope))
+    framed = jnp.pad(planes, ((0, 0), (1, 1), (1, 1), (0, 0)))
+    windows = [framed[:, a : a + TH, b : b + TW, :].reshape(-1, C) for a in range(3) for b in range(3)]
+    taps = jnp.concatenate(windows, axis=1).T
+    outgoing, slope, taps = lax.optimization_barrier((outgoing, slope, taps))
 
     upstream = jnp.take(upstream_slots, slot_ids, axis=0, mode="clip")
     mask = occupancy.astype(jnp.float32)
@@ -112,7 +115,7 @@
     grad_pre = grad_pre * mask[:, None, None, None]
     grad_pre = grad_pre.astype(jnp.bfloat16).reshape(count * TD, TH, TW, C)
     back = conv_input_grad(grad_pre, kernel)
-    wgrad = conv_kernel_grad(planes, grad_pre).reshape(9 * C, C)
+    wgrad = jnp.dot(taps, grad_pre.reshape(-1, C), preferred_element_type=jnp.float32)
     back = back * plane_mask[:, None, None, None]
     input_grad = back.astype(jnp.bfloat16).reshape(count, TD, TH, TW * C)
 

time: 148 us -> 157 us (1.061)
  local copies, waits for them, and re-layouts: 15.8 us -> 36.1 us
  waiting for transfers between devices: 22.5 us -> 5.85 us
  blocking collectives: 65.7 us -> 69.6 us
    all_to_all x1, waiting for transfers between devices: 16.1 us -> 0.01 us  [local(): lax.all_to_all(cotangent, 'slab', split_axis=0, concat_axis=0, tiled=True)]
    concatenate x0 -> x1, local copies, waits for them, and re-layouts: none -> 11.7 us  [local(): taps = jnp.concatenate(windows, axis=1).T]
    slice x0 -> x1, local copies, waits for them, and re-layouts: none -> 6.88 us  [local(): framed[:, a:a + TH, b:b + TW, :].reshape(-1, C)]
    dot_general x0 -> x1, matrix products: none -> 4.04 us  [local(): jnp.dot(taps, grad_pre.reshape(-1, C), preferred_element_type=jnp.float32)]
    all_to_all x1, blocking collectives: 45.8 us -> 49.4 us  [local(): lax.all_to_all(payload, 'slab', split_axis=0, concat_axis=0, tiled=True)]
    conv_general_dilated x1 -> x0, matrix products: 2.77 us -> none  [conv_kernel_grad(): lax.conv_general_dilated(planes, grad_planes, (1, 1), ((1, 1), (1, 1)), d...]
    reshape x0 -> x2, local copies, waits for them, and re-layouts: none -> 1.64 us  [the longest x1 1.52 us: local(): framed[:, a:a + TH, b:b + TW, :].reshape(-1, C)]
  transfers between devices with their start and end apart: 2 -> 2, of which waited for: 2 -> 1; matrix products, arithmetic and copies ran while one was open for 13% -> 26% of each run, Pallas kernels for 0% -> 0%
where the time goes in v8:
time: 157 us; the launch traced here: 156 us
  blocking collectives  69.6 us (44%)
  local copies, waits for them, and re-layouts  36.1 us (23%)
  starting transfers between devices  30.5 us (19%)
  matrix products  12.1 us (8%)
  waiting for transfers between devices  5.85 us (4%)
    all_to_all x1, blocking collectives, local(): lax.all_to_all(payload, 'slab', split_axis=0, concat_axis=0, tiled=True)  49.4 us
    all_to_all x1, starting transfers between devices, local(): lax.all_to_all(cotangent, 'slab', split_axis=0, concat_axis=0, tiled=True)  23.5 us
    all_to_all x1, blocking collectives, sent_to_all(): lax.all_to_all(jnp.broadcast_to(x[None], (size, *x.shape)), axis, 0, 0, t...  20.2 us
    concatenate x1, local copies, waits for them, and re-layouts, local(): taps = jnp.concatenate(windows, axis=1).T  11.7 us
    all_to_all x1, starting transfers between devices, sent_to_all(): lax.all_to_all(jnp.broadcast_to(x[None], (size, *x.shape)), axis, 0, 0, t...  7 us
    slice x1, local copies, waits for them, and re-layouts, local(): framed[:, a:a + TH, b:b + TW, :].reshape(-1, C)  6.88 us
    all_to_all x1, waiting for transfers between devices, sent_to_all(): lax.all_to_all(jnp.broadcast_to(x[None], (size, *x.shape)), axis, 0, 0, t...  5.85 us
    dot_general x1, matrix products, local(): jnp.dot(taps, grad_pre.reshape(-1, C), preferred_element_type=jnp.float32)  4.04 us
  transfers between devices with their start and end apart: 2, of which 1 were waited for; matrix products, arithmetic and copies ran while one was open for 26% of the time, Pallas kernels for 0%

profile of v8, /device:TPU:1, one launch (start us, length us, event | category | flops | bytes accessed | tf_op | source)
XLA Modules:
  0.0 156.1 jit_solution(3009617390652185209)
XLA Ops:
  0.6 0.0 copy-start.2
  0.6 0.0 copy-start.3
  0.6 23.5 %all-to-all-start = ((bf16[64,2,8,512]{3,2,1,0:T(8,128)(2,1)}), bf16[64,2,8,512]{3,2,1,0:T(8,128)(2,1)}, u32[]{:S(2)}, u32[]{:S(2)}) async-start(bf16[64,2,8,512]{3,2,1,0:T(8,128)(2,1)} %param.9), calls=%async_computation | async-start | bytes 2097152 | tf_op jit(solution)/shard_map/all_to_all | solution.py:94
  24.1 0.0 copy-done.2
  24.1 0.5 reshape.101
  24.7 0.0 copy-start.1
  24.7 1.5 reshape.109
  26.2 0.0 copy-done.3
  26.2 0.1 copy.42
  26.3 3.6 %add_multiply_fusion = (f32[64,8,8,64]{3,0,2,1:T(8,128)}, bf16[64,8,8,64]{3,0,2,1:T(8,128)(2,1)S(1)}) fusion(bf16[3,3,64,64]{3,2,1,0:T(8,128)(2,1)S(1)} %bitcast.64, bf16[64,8,8,64]{3,2,1,0:T(8,128)(2,1)S(1)} %reshape.101), kind=kOutput, calls=%fused_computation.10 | convolution fusion | flops 256114688 | bytes 2170880 | tf_op jit(solution)/shard_map/conv_general_dilated | solution.py:46
  30.0 0.0 copy-done.1
  30.0 0.7 copy.44
  30.7 1.4 reshape.103
  32.1 2.8 %copy.46 = f32[64,8,8,64]{3,2,1,0:T(8,128)S(1)} copy(f32[64,8,8,64]{3,0,2,1:T(8,128)} %get-tuple-element.23) | data formatting | bytes 2097152 | tf_op jit(solution)/shard_map/mul | solution.py:101
  34.9 0.0 copy-start.4
  34.9 1.5 reshape.104
  36.4 0.0 copy-done.4
  36.4 6.9 %pad_slice_fusion = (bf16[64,8,8,64]{3,2,1,0:T(8,128)(2,1)S(1)}, bf16[64,8,8,64]{3,2,1,0:T(8,128)(2,1)S(1)}, bf16[64,8,8,64]{3,2,1,0:T(8,128)(2,1)S(1)}, bf16[64...) fusion(bf16[64,8,8,64]{3,2,1,0:T(8,128)(2,1)} %copy-done.1), kind=kLoop, calls=%fused_computation.1 | loop fusion | bytes 4718592 | tf_op jit(solution)/shard_map/slice | solution.py:107
  43.3 0.0 copy-start.5
  43.3 11.7 %concatenate.10 = bf16[4096,576]{1,0:T(8,128)(2,1)} concatenate(bf16[4096,64]{1,0:T(8,128)(2,1)} %bitcast.57, bf16[4096,64]{1,0:T(8,128)(2,1)S(1)} %bitcast.51, bf16[4096,64]{1,0:T(8,128)(2,1)S(1)} %bitcast.52, bf16[4096,64]{1,0:T(8,128)(2,1)} %bitcast.53, bf16[4096,64]{1,0:T(8,128)(2,1)} %reshape.109, bf16[4096,64]{1,0:T(8,128)(2,1)} %bitcast.54, bf16[4096,64]{1,0:T(8,128)(2,1)} %bitcast.55, ...), dimensions={1} | concatenate | bytes 9437184 | tf_op jit(solution)/shard_map/concatenate | solution.py:108
  55.0 0.0 copy-done.5
  55.0 0.2 convert_reduce_fusion
  55.2 0.0 copy-start
  55.2 1.7 %convolution_convert_fusion = bf16[64,2,8,512]{3,0,2,1:T(8,128)(2,1)S(1)} fusion(bf16[32,2,8,512]{3,2,1,0:T(8,128)(2,1)} %reshape.103, s32[32]{0:T(128)S(1)} %multiply_add_fusion, pred[32]{0:T(512)(128)(4,1)S(1)} %broadcast_compare_fusion), kind=kOutput, calls=%fused_computation.13 | convolution fusion | flops 34082816 | bytes 1573024 | tf_op jit(solution)/shard_map/sk,kdhx->sdhx/dot_general | solution.py:102
  56.9 0.6 copy.47
  57.5 0.0 all-to-all-done
  57.5 1.8 %gather_fusion = bf16[32,2,8,512]{3,2,1,0:T(8,128)(2,1)S(1)} fusion(bf16[64,2,8,512]{3,2,1,0:T(8,128)(2,1)} %all-to-all-done, s32[1024]{0:T(1024)S(1)} %pad_clamp_fusion), kind=kCustom, calls=%fused_computation | custom fusion | bytes 1048704 | tf_op jit(solution)/shard_map/jit(_take)/gather | solution.py:111
  59.3 0.0 copy-done
  59.3 0.2 multiply_convert_fusion.2
  59.5 0.5 reshape_reshape.4
  60.0 4.0 %fusion.15 = f32[576,64]{1,0:T(8,128)S(1)} fusion(bf16[576,4096]{0,1:T(8,128)(2,1)} %bitcast.49, bf16[4096,64]{1,0:T(8,128)(2,1)S(1)} %reshape_reshape.4), kind=kOutput, calls=%fused_computation.44 | convolution fusion | flops 301989888 | bytes 5390336 | tf_op jit(solution)/shard_map/dot_general | solution.py:118
  64.1 0.1 reshape.115
  64.3 0.1 copy.56
  64.4 0.1 pad_maximum_fusion
  64.5 49.4 %all_to_all.22 = bf16[32,5,8,512]{3,2,1,0:T(8,128)(2,1)S(1)} all-to-all(bf16[32,5,8,512]{3,2,1,0:T(8,128)(2,1)S(1)} %pad_maximum_fusion), channel_id=1, replica_groups=mesh['grp'=32,'slab'=32] {'slab'}, dimensions={0} | all-to-all | bytes 2621440 | tf_op jit(solution)/shard_map/all_to_all | solution.py:133
  113.9 0.1 copy.57
  114.1 0.1 broadcast_in_dim.9
  114.2 20.2 %all_to_all.23 = f32[32,1,1152]{2,1,0:T(1,128)S(1)} all-to-all(f32[32,1,1152]{2,1,0:T(1,128)S(1)} %broadcast_in_dim.9), channel_id=1, replica_groups=mesh['grp'=32,'slab'=32] {'grp'}, dimensions={0} | all-to-all | bytes 294912 | tf_op jit(solution)/shard_map/all_to_all | solution.py:27
  134.4 0.1 reduce_sum.42
  134.5 0.7 broadcast_in_dim.10
  135.2 7.0 %all-to-all-start.3 = ((f32[32,1,1152]{2,1,0:T(1,128)}), f32[32,1,1152]{2,1,0:T(1,128)S(1)}, u32[]{:S(2)}, u32[]{:S(2)}) async-start(f32[32,1,1152]{2,1,0:T(1,128)} %broadcast_in_dim.10), calls=%async_computation.3 | async-start | bytes 294912 | tf_op jit(solution)/shard_map/all_to_all | solution.py:27
  142.2 0.1 broadcast_in_dim.8
  142.3 0.1 mul.64
  142.4 0.5 reshape.118
  142.9 2.8 %multiply_convert_fusion = bf16[64,8,8,64]{3,0,2,1:T(8,128)(2,1)S(1)} fusion(bf16[3,3,64,64]{3,2,1,0:T(8,128)(2,1)S(1)} %bitcast.65, bf16[64,8,8,64]{3,2,1,0:T(8,128)(2,1)S(1)} %reshape.118, f32[64]{0:T(128)S(1)} %mul.64), kind=kOutput, calls=%fused_computation.9 | convolution fusion | flops 254279680 | bytes 1122560 | tf_op jit(solution)/shard_map/conv_general_dilated | solution.py:58
  145.7 0.7 copy.50
  146.4 1.4 reshape.119
  147.8 1.1 slice.55
  148.9 5.8 %all-to-all-done.3 = f32[32,1,1152]{2,1,0:T(1,128)S(1)} async-done(((f32[32,1,1152]{2,1,0:T(1,128)}), f32[32,1,1152]{2,1,0:T(1,128)S(1)}, u32[]{:S(2)}, u32[]{:S(2)}) %all-to-all-start.3) | async-done | bytes 147488 | tf_op jit(solution)/shard_map/all_to_all | solution.py:27
  154.8 0.4 multiply_reduce_fusion
  155.2 0.1 mul.69
  155.3 0.8 copy.52
  (11 shorter events, 0.1 us)
Async XLA Ops:
  0.6 23.5 %copy-start.2 = (bf16[32,2,8,512]{3,2,1,0:T(8,128)(2,1)S(1)}, bf16[32,2,8,512]{3,2,1,0:T(8,128)(2,1)}, u32[]{:S(2)}) copy-start(bf16[32,2,8,512]{3,2,1,0:T(8,128)(2,1)} %param.5) | copy-start | bytes 1572868
  0.6 25.6 %copy-start.3 = (bf16[576,64]{0,1:T(8,128)(2,1)S(1)}, bf16[576,64]{0,1:T(8,128)(2,1)}, u32[]{:S(2)}) copy-start(bf16[576,64]{0,1:T(8,128)(2,1)} %param.6) | copy-start | bytes 221188
  0.6 56.9 %all-to-all-start = ((bf16[64,2,8,512]{3,2,1,0:T(8,128)(2,1)}), bf16[64,2,8,512]{3,2,1,0:T(8,128)(2,1)}, u32[]{:S(2)}, u32[]{:S(2)}) async-start(bf16[64,2,8,512]{3,2,1,0:T(8,128)(2,1)} %param.9), calls=%async_computation | async-start | bytes 2097152 | tf_op jit(solution)/shard_map/all_to_all | solution.py:94
  24.7 5.3 %copy-start.1 = (bf16[64,8,8,64]{3,2,1,0:T(8,128)(2,1)}, bf16[64,8,8,64]{3,2,1,0:T(8,128)(2,1)S(1)}, u32[]{:S(2)}) copy-start(bf16[64,8,8,64]{3,2,1,0:T(8,128)(2,1)S(1)} %reshape.101) | copy-start | bytes 1572868
  34.9 1.5 copy-start.4
  43.3 11.7 %copy-start.5 = (s32[32,1]{0,1:T(1,128)S(1)}, s32[32,1]{0,1:T(1,128)}, u32[]{:S(2)}) copy-start(s32[32,1]{0,1:T(1,128)} %param.7) | copy-start | bytes 388
  55.2 4.1 %copy-start = (f32[32,2,8,512]{3,2,1,0:T(8,128)S(1)}, f32[32,2,8,512]{3,2,1,0:T(8,128)}, u32[]{:S(2)}) copy-start(f32[32,2,8,512]{3,2,1,0:T(8,128)} %reshape.104) | copy-start | bytes 3145732
  135.2 19.5 %all-to-all-start.3 = ((f32[32,1,1152]{2,1,0:T(1,128)}), f32[32,1,1152]{2,1,0:T(1,128)S(1)}, u32[]{:S(2)}, u32[]{:S(2)}) async-start(f32[32,1,1152]{2,1,0:T(1,128)} %broadcast_in_dim.10), calls=%async_computation.3 | async-start | bytes 294912 | tf_op jit(solution)/shard_map/all_to_all | solution.py:27

commit v9 on v7

--- a/solution.py
+++ b/solution.py
@@ -105,9 +105,7 @@
     slope = slope.reshape(count, TD, TH, TW * C)
     outgoing, slope = lax.optimization_barrier((outgoing, slope))
 
-    upstream = jnp.einsum(
-        "sk,sdhx->kdhx", placer, upstream_slots, preferred_element_type=jnp.float32
-    )
+    upstream = jnp.take(upstream_slots, slot_ids, axis=0, mode="clip")
     mask = occupancy.astype(jnp.float32)
     plane_mask = jnp.repeat(mask, TD)
     grad_pre = upstream.astype(jnp.float32) * slope
@@ -118,7 +116,7 @@
     back = back * plane_mask[:, None, None, None]
     input_grad = back.astype(jnp.bfloat16).reshape(count, TD, TH, TW * C)
 
-    flat_w = wgrad.reshape(n_slab, -1)
+    flat_w = wgrad.T.reshape(n_slab, -1)
     high = lax.reduce_precision(flat_w, exponent_bits=8, mantissa_bits=7)
     low = flat_w - high
     share_width = flat_w.shape[1]
@@ -135,7 +133,7 @@
     share = jnp.sum(got[:, :share_width], axis=0) + jnp.sum(got[:, share_width:], axis=0)
     scale = 1.0 / math.sqrt(per_owner * n_group * n_slab * TD * TH * TW)
     share = over_copies(share, "grp") * scale
-    summed = gathered_copies(share, "slab", 0).reshape(9 * C, C)
+    summed = gathered_copies(share, "slab", 0).reshape(C, 9 * C).T
     return (activations, input_grad, summed)
 
 

time: 149 us -> 148 us (level)
  matrix products: 14.1 us -> 11.1 us
    dot_general x1 -> x0, matrix products: 3 us -> none  [local(): jnp.einsum('sk,sdhx->kdhx', placer, upstream_slots, preferred_element_typ...]
    gather x0 -> x1, local copies, waits for them, and re-layouts: none -> 1.8 us  [local(): upstream = jnp.take(upstream_slots, slot_ids, axis=0, mode='clip')]
where the time goes in v9:
time: 148 us; the launch traced here: 147 us
  blocking collectives  65.7 us (44%)
  starting transfers between devices  30.4 us (21%)
  waiting for transfers between devices  22.5 us (15%)
  local copies, waits for them, and re-layouts  15.7 us (11%)
  matrix products  11.1 us (8%)
    all_to_all x1, blocking collectives, local(): lax.all_to_all(payload, 'slab', split_axis=0, concat_axis=0, tiled=True)  45.8 us
    all_to_all x1, starting transfers between devices, local(): lax.all_to_all(cotangent, 'slab', split_axis=0, concat_axis=0, tiled=True)  23.5 us
    all_to_all x1, blocking collectives, sent_to_all(): lax.all_to_all(jnp.broadcast_to(x[None], (size, *x.shape)), axis, 0, 0, t...  19.9 us
    all_to_all x1, waiting for transfers between devices, local(): lax.all_to_all(cotangent, 'slab', split_axis=0, concat_axis=0, tiled=True)  16.1 us
    all_to_all x1, starting transfers between devices, sent_to_all(): lax.all_to_all(jnp.broadcast_to(x[None], (size, *x.shape)), axis, 0, 0, t...  6.96 us
    all_to_all x1, waiting for transfers between devices, sent_to_all(): lax.all_to_all(jnp.broadcast_to(x[None], (size, *x.shape)), axis, 0, 0, t...  6.39 us
    conv_general_dilated x1, matrix products, conv_forward(): lax.conv_general_dilated(planes, kernel, (1, 1), ((1, 1), (1, 1)), dimens...  3.98 us
  transfers between devices with their start and end apart: 2, of which 2 were waited for; matrix products, arithmetic and copies ran while one was open for 13% of the time, Pallas kernels for 0%

profile of v9, /device:TPU:1, one launch (start us, length us, event | category | flops | bytes accessed | tf_op | source)
XLA Modules:
  0.0 147.4 jit_solution(4188485551176346411)
XLA Ops:
  0.6 0.0 copy-start.1
  0.6 23.5 %all-to-all-start = ((bf16[64,2,8,512]{3,2,1,0:T(8,128)(2,1)}), bf16[64,2,8,512]{3,2,1,0:T(8,128)(2,1)}, u32[]{:S(2)}, u32[]{:S(2)}) async-start(bf16[64,2,8,512]{3,2,1,0:T(8,128)(2,1)} %param.9), calls=%async_computation | async-start | bytes 2097152 | tf_op jit(solution)/shard_map/all_to_all | solution.py:94
  24.1 0.0 copy-done.1
  24.1 0.0 copy-start.2
  24.1 0.5 reshape.77
  24.7 1.2 copy.53
  25.9 0.0 copy-done.2
  25.9 0.0 copy-start
  25.9 0.1 copy.47
  26.1 4.0 %add_multiply_fusion = (f32[64,8,8,64]{3,0,2,1:T(8,128)}, bf16[64,8,8,64]{3,0,2,1:T(8,128)(2,1)S(1)}) fusion(bf16[64,8,8,64]{0,3,2,1:T(8,128)(2,1)S(1)} %copy.53, bf16[3,3,64,64]{3,2,1,0:T(8,128)(2,1)S(1)} %bitcast.48), kind=kOutput, calls=%fused_computation.2 | convolution fusion | flops 256114688 | bytes 2170880 | tf_op jit(solution)/shard_map/conv_general_dilated | solution.py:46
  30.0 0.0 copy-done
  30.0 0.7 copy.49
  30.7 1.4 reshape.79
  32.1 2.8 %copy.51 = f32[64,8,8,64]{3,2,1,0:T(8,128)S(1)} copy(f32[64,8,8,64]{3,0,2,1:T(8,128)} %get-tuple-element.9) | data formatting | bytes 2097152 | tf_op jit(solution)/shard_map/mul | solution.py:101
  34.9 0.0 copy-start.3
  35.0 0.0 copy-start.4
  35.0 0.5 reshape.80
  35.5 0.1 copy-done.3
  35.6 0.0 copy-done.4
  35.6 0.2 convert_reduce_fusion
  35.8 1.6 %convolution_convert_fusion = bf16[64,2,8,512]{3,0,2,1:T(8,128)(2,1)S(1)} fusion(bf16[32,2,8,512]{3,2,1,0:T(8,128)(2,1)} %reshape.79, s32[32]{0:T(128)S(1)} %multiply_add_fusion, pred[32]{0:T(512)(128)(4,1)S(1)} %broadcast_compare_fusion), kind=kOutput, calls=%fused_computation.5 | convolution fusion | flops 34082816 | bytes 1573024 | tf_op jit(solution)/shard_map/sk,kdhx->sdhx/dot_general | solution.py:102
  37.4 0.6 copy.52
  38.0 16.1 %all-to-all-done = bf16[64,2,8,512]{3,2,1,0:T(8,128)(2,1)} async-done(((bf16[64,2,8,512]{3,2,1,0:T(8,128)(2,1)}), bf16[64,2,8,512]{3,2,1,0:T(8,128)(2,1)}, u32[]{:S(2)}, u32[]{:S(2)}) %all-to-all-start) | async-done | bytes 1048608 | tf_op jit(solution)/shard_map/all_to_all | solution.py:94
  54.1 1.8 %gather_fusion = bf16[32,2,8,512]{3,2,1,0:T(8,128)(2,1)S(1)} fusion(bf16[64,2,8,512]{3,2,1,0:T(8,128)(2,1)} %all-to-all-done, s32[1024]{0:T(1024)S(1)} %pad_clamp_fusion), kind=kCustom, calls=%fused_computation | custom fusion | bytes 1048704 | tf_op jit(solution)/shard_map/jit(_take)/gather | solution.py:108
  55.9 0.2 multiply_convert_fusion.2
  56.1 0.5 reshape.82
  56.6 2.8 %fusion.1 = f32[3,3,64,64]{3,2,1,0:T(8,128)S(1)} fusion(bf16[64,8,8,64]{0,3,2,1:T(8,128)(2,1)} %copy-done, bf16[64,8,8,64]{3,2,1,0:T(8,128)(2,1)S(1)} %reshape.82), kind=kOutput, calls=%fused_computation.9 | convolution fusion | flops 253755392 | bytes 1196032 | tf_op jit(solution)/shard_map/conv_general_dilated | solution.py:69
  59.4 0.1 copy.55
  59.6 0.1 reshape.84
  59.7 0.1 copy.61
  59.8 0.1 pad_maximum_fusion
  59.9 45.8 %all_to_all.22 = bf16[32,5,8,512]{3,2,1,0:T(8,128)(2,1)S(1)} all-to-all(bf16[32,5,8,512]{3,2,1,0:T(8,128)(2,1)S(1)} %pad_maximum_fusion), channel_id=1, replica_groups=mesh['grp'=32,'slab'=32] {'slab'}, dimensions={0} | all-to-all | bytes 2621440 | tf_op jit(solution)/shard_map/all_to_all | solution.py:130
  105.8 0.1 copy.62
  106.0 0.1 broadcast_in_dim.9
  106.0 19.9 %all_to_all.23 = f32[32,1,1152]{2,1,0:T(1,128)S(1)} all-to-all(f32[32,1,1152]{2,1,0:T(1,128)S(1)} %broadcast_in_dim.9), channel_id=1, replica_groups=mesh['grp'=32,'slab'=32] {'grp'}, dimensions={0} | all-to-all | bytes 294912 | tf_op jit(solution)/shard_map/all_to_all | solution.py:27
  125.9 0.1 reduce_sum.42
  126.1 0.7 broadcast_in_dim.10
  126.8 7.0 %all-to-all-start.3 = ((f32[32,1,1152]{2,1,0:T(1,128)}), f32[32,1,1152]{2,1,0:T(1,128)S(1)}, u32[]{:S(2)}, u32[]{:S(2)}) async-start(f32[32,1,1152]{2,1,0:T(1,128)} %broadcast_in_dim.10), calls=%async_computation.3 | async-start | bytes 294912 | tf_op jit(solution)/shard_map/all_to_all | solution.py:27
  133.8 0.1 broadcast_in_dim.8
  133.8 0.1 mul.65
  133.9 2.7 %multiply_convert_fusion = bf16[64,8,8,64]{3,0,2,1:T(8,128)(2,1)S(1)} fusion(bf16[3,3,64,64]{3,2,1,0:T(8,128)(2,1)S(1)} %bitcast.49, f32[64]{0:T(128)S(1)} %mul.65, bf16[64,8,8,64]{3,2,1,0:T(8,128)(2,1)S(1)} %reshape.82), kind=kOutput, calls=%fused_computation.1 | convolution fusion | flops 254279680 | bytes 1122560 | tf_op jit(solution)/shard_map/conv_general_dilated | solution.py:58
  136.7 0.7 copy.57
  137.4 1.4 reshape.87
  138.8 1.1 slice.22
  139.9 6.4 %all-to-all-done.3 = f32[32,1,1152]{2,1,0:T(1,128)S(1)} async-done(((f32[32,1,1152]{2,1,0:T(1,128)}), f32[32,1,1152]{2,1,0:T(1,128)S(1)}, u32[]{:S(2)}, u32[]{:S(2)}) %all-to-all-start.3) | async-done | bytes 147488 | tf_op jit(solution)/shard_map/all_to_all | solution.py:27
  146.3 0.3 reduce.1
  146.7 0.8 reshape_reshape.3
  (12 shorter events, 0.1 us)
Async XLA Ops:
  0.6 23.5 %copy-start.1 = (bf16[32,2,8,512]{3,2,1,0:T(8,128)(2,1)S(1)}, bf16[32,2,8,512]{3,2,1,0:T(8,128)(2,1)}, u32[]{:S(2)}) copy-start(bf16[32,2,8,512]{3,2,1,0:T(8,128)(2,1)} %param.5) | copy-start | bytes 1572868
  0.6 53.5 %all-to-all-start = ((bf16[64,2,8,512]{3,2,1,0:T(8,128)(2,1)}), bf16[64,2,8,512]{3,2,1,0:T(8,128)(2,1)}, u32[]{:S(2)}, u32[]{:S(2)}) async-start(bf16[64,2,8,512]{3,2,1,0:T(8,128)(2,1)} %param.9), calls=%async_computation | async-start | bytes 2097152 | tf_op jit(solution)/shard_map/all_to_all | solution.py:94
  24.1 1.8 %copy-start.2 = (bf16[576,64]{0,1:T(8,128)(2,1)S(1)}, bf16[576,64]{0,1:T(8,128)(2,1)}, u32[]{:S(2)}) copy-start(bf16[576,64]{0,1:T(8,128)(2,1)} %param.6) | copy-start | bytes 221188
  25.9 4.1 %copy-start = (bf16[64,8,8,64]{0,3,2,1:T(8,128)(2,1)}, bf16[64,8,8,64]{0,3,2,1:T(8,128)(2,1)S(1)}, u32[]{:S(2)}) copy-start(bf16[64,8,8,64]{0,3,2,1:T(8,128)(2,1)S(1)} %copy.53) | copy-start | bytes 1572868
  34.9 0.7 copy-start.3
  35.0 0.7 copy-start.4
  126.8 19.5 %all-to-all-start.3 = ((f32[32,1,1152]{2,1,0:T(1,128)}), f32[32,1,1152]{2,1,0:T(1,128)S(1)}, u32[]{:S(2)}, u32[]{:S(2)}) async-start(f32[32,1,1152]{2,1,0:T(1,128)} %broadcast_in_dim.10), calls=%async_computation.3 | async-start | bytes 294912 | tf_op jit(solution)/shard_map/all_to_all | solution.py:27

commit v10 on v9

--- a/solution.py
+++ b/solution.py
@@ -116,7 +116,8 @@
     back = back * plane_mask[:, None, None, None]
     input_grad = back.astype(jnp.bfloat16).reshape(count, TD, TH, TW * C)
 
-    flat_w = wgrad.T.reshape(n_slab, -1)
+    scale = 1.0 / math.sqrt(per_owner * n_group * n_slab * TD * TH * TW)
+    flat_w = (wgrad * scale).T.reshape(n_slab, -1)
     high = lax.reduce_precision(flat_w, exponent_bits=8, mantissa_bits=7)
     low = flat_w - high
     share_width = flat_w.shape[1]
@@ -131,8 +132,7 @@
     activations = arrived[:, : capacity * TD].reshape(outgoing.shape)
     got = arrived[:, capacity * TD :].reshape(n_slab, -1)[:, : 2 * share_width].astype(jnp.float32)
     share = jnp.sum(got[:, :share_width], axis=0) + jnp.sum(got[:, share_width:], axis=0)
-    scale = 1.0 / math.sqrt(per_owner * n_group * n_slab * TD * TH * TW)
-    share = over_copies(share, "grp") * scale
+    share = over_copies(share, "grp")
     summed = gathered_copies(share, "slab", 0).reshape(C, 9 * C).T
     return (activations, input_grad, summed)
 

time: 148 us -> 148 us (level)
  no operation moved by 1% of the time
where the time goes in v10:
time: 148 us; the launch traced here: 147 us
  blocking collectives  65.7 us (44%)
  starting transfers between devices  30.4 us (21%)
  waiting for transfers between devices  22.5 us (15%)
  local copies, waits for them, and re-layouts  15.7 us (11%)
  matrix products  11.1 us (8%)
    all_to_all x1, blocking collectives, local(): lax.all_to_all(payload, 'slab', split_axis=0, concat_axis=0, tiled=True)  45.8 us
    all_to_all x1, starting transfers between devices, local(): lax.all_to_all(cotangent, 'slab', split_axis=0, concat_axis=0, tiled=True)  23.5 us
    all_to_all x1, blocking collectives, sent_to_all(): lax.all_to_all(jnp.broadcast_to(x[None], (size, *x.shape)), axis, 0, 0, t...  19.9 us
    all_to_all x1, waiting for transfers between devices, local(): lax.all_to_all(cotangent, 'slab', split_axis=0, concat_axis=0, tiled=True)  16.1 us
    all_to_all x1, starting transfers between devices, sent_to_all(): lax.all_to_all(jnp.broadcast_to(x[None], (size, *x.shape)), axis, 0, 0, t...  6.96 us
    all_to_all x1, waiting for transfers between devices, sent_to_all(): lax.all_to_all(jnp.broadcast_to(x[None], (size, *x.shape)), axis, 0, 0, t...  6.39 us
    conv_general_dilated x1, matrix products, conv_forward(): lax.conv_general_dilated(planes, kernel, (1, 1), ((1, 1), (1, 1)), dimens...  3.98 us
  transfers between devices with their start and end apart: 2, of which 2 were waited for; matrix products, arithmetic and copies ran while one was open for 13% of the time, Pallas kernels for 0%

profile of v10, /device:TPU:1, one launch (start us, length us, event | category | flops | bytes accessed | tf_op | source)
XLA Modules:
  0.0 147.4 jit_solution(13588212807080322693)
XLA Ops:
  0.6 0.0 copy-start.1
  0.6 23.5 %all-to-all-start = ((bf16[64,2,8,512]{3,2,1,0:T(8,128)(2,1)}), bf16[64,2,8,512]{3,2,1,0:T(8,128)(2,1)}, u32[]{:S(2)}, u32[]{:S(2)}) async-start(bf16[64,2,8,512]{3,2,1,0:T(8,128)(2,1)} %param.9), calls=%async_computation | async-start | bytes 2097152 | tf_op jit(solution)/shard_map/all_to_all | solution.py:94
  24.1 0.0 copy-done.1
  24.1 0.0 copy-start.2
  24.1 0.5 reshape.74
  24.7 1.2 copy.53
  25.9 0.0 copy-done.2
  25.9 0.0 copy-start
  25.9 0.1 copy.47
  26.1 4.0 %add_multiply_fusion = (f32[64,8,8,64]{3,0,2,1:T(8,128)}, bf16[64,8,8,64]{3,0,2,1:T(8,128)(2,1)S(1)}) fusion(bf16[64,8,8,64]{0,3,2,1:T(8,128)(2,1)S(1)} %copy.53, bf16[3,3,64,64]{3,2,1,0:T(8,128)(2,1)S(1)} %bitcast.48), kind=kOutput, calls=%fused_computation.2 | convolution fusion | flops 256114688 | bytes 2170880 | tf_op jit(solution)/shard_map/conv_general_dilated | solution.py:46
  30.0 0.0 copy-done
  30.0 0.7 copy.49
  30.7 1.4 reshape.76
  32.1 2.8 %copy.51 = f32[64,8,8,64]{3,2,1,0:T(8,128)S(1)} copy(f32[64,8,8,64]{3,0,2,1:T(8,128)} %get-tuple-element.9) | data formatting | bytes 2097152 | tf_op jit(solution)/shard_map/mul | solution.py:101
  34.9 0.0 copy-start.3
  35.0 0.0 copy-start.4
  35.0 0.5 reshape.77
  35.5 0.1 copy-done.3
  35.6 0.0 copy-done.4
  35.6 0.2 convert_reduce_fusion
  35.8 1.6 %convolution_convert_fusion = bf16[64,2,8,512]{3,0,2,1:T(8,128)(2,1)S(1)} fusion(bf16[32,2,8,512]{3,2,1,0:T(8,128)(2,1)} %reshape.76, s32[32]{0:T(128)S(1)} %multiply_add_fusion, pred[32]{0:T(512)(128)(4,1)S(1)} %broadcast_compare_fusion), kind=kOutput, calls=%fused_computation.5 | convolution fusion | flops 34082816 | bytes 1573024 | tf_op jit(solution)/shard_map/sk,kdhx->sdhx/dot_general | solution.py:102
  37.4 0.6 copy.52
  38.0 16.1 %all-to-all-done = bf16[64,2,8,512]{3,2,1,0:T(8,128)(2,1)} async-done(((bf16[64,2,8,512]{3,2,1,0:T(8,128)(2,1)}), bf16[64,2,8,512]{3,2,1,0:T(8,128)(2,1)}, u32[]{:S(2)}, u32[]{:S(2)}) %all-to-all-start) | async-done | bytes 1048608 | tf_op jit(solution)/shard_map/all_to_all | solution.py:94
  54.1 1.8 %gather_fusion = bf16[32,2,8,512]{3,2,1,0:T(8,128)(2,1)S(1)} fusion(bf16[64,2,8,512]{3,2,1,0:T(8,128)(2,1)} %all-to-all-done, s32[1024]{0:T(1024)S(1)} %pad_clamp_fusion), kind=kCustom, calls=%fused_computation | custom fusion | bytes 1048704 | tf_op jit(solution)/shard_map/jit(_take)/gather | solution.py:108
  55.9 0.2 multiply_convert_fusion.2
  56.1 0.5 reshape.79
  56.6 2.8 %convolution_multiply_fusion = f32[3,3,64,64]{3,2,1,0:T(8,128)S(1)} fusion(bf16[64,8,8,64]{0,3,2,1:T(8,128)(2,1)} %copy-done, bf16[64,8,8,64]{3,2,1,0:T(8,128)(2,1)S(1)} %reshape.79), kind=kOutput, calls=%fused_computation.7 | convolution fusion | flops 253792256 | bytes 1196032 | tf_op jit(solution)/shard_map/conv_general_dilated | solution.py:69
  59.4 0.1 copy.55
  59.6 0.1 reshape.80
  59.7 0.1 copy.61
  59.8 0.1 pad_maximum_fusion
  59.9 45.8 %all_to_all.22 = bf16[32,5,8,512]{3,2,1,0:T(8,128)(2,1)S(1)} all-to-all(bf16[32,5,8,512]{3,2,1,0:T(8,128)(2,1)S(1)} %pad_maximum_fusion), channel_id=1, replica_groups=mesh['grp'=32,'slab'=32] {'slab'}, dimensions={0} | all-to-all | bytes 2621440 | tf_op jit(solution)/shard_map/all_to_all | solution.py:131
  105.8 0.1 copy.62
  106.0 0.1 broadcast_in_dim.9
  106.0 19.9 %all_to_all.23 = f32[32,1,1152]{2,1,0:T(1,128)S(1)} all-to-all(f32[32,1,1152]{2,1,0:T(1,128)S(1)} %broadcast_in_dim.9), channel_id=1, replica_groups=mesh['grp'=32,'slab'=32] {'grp'}, dimensions={0} | all-to-all | bytes 294912 | tf_op jit(solution)/shard_map/all_to_all | solution.py:27
  125.9 0.1 reduce_sum.42
  126.0 0.7 broadcast_in_dim.10
  126.8 7.0 %all-to-all-start.3 = ((f32[32,1,1152]{2,1,0:T(1,128)}), f32[32,1,1152]{2,1,0:T(1,128)S(1)}, u32[]{:S(2)}, u32[]{:S(2)}) async-start(f32[32,1,1152]{2,1,0:T(1,128)} %broadcast_in_dim.10), calls=%async_computation.3 | async-start | bytes 294912 | tf_op jit(solution)/shard_map/all_to_all | solution.py:27
  133.8 0.1 broadcast_in_dim.8
  133.8 0.1 mul.67
  133.9 2.8 %multiply_convert_fusion = bf16[64,8,8,64]{3,0,2,1:T(8,128)(2,1)S(1)} fusion(bf16[3,3,64,64]{3,2,1,0:T(8,128)(2,1)S(1)} %bitcast.49, f32[64]{0:T(128)S(1)} %mul.67, bf16[64,8,8,64]{3,2,1,0:T(8,128)(2,1)S(1)} %reshape.79), kind=kOutput, calls=%fused_computation.1 | convolution fusion | flops 254279680 | bytes 1122560 | tf_op jit(solution)/shard_map/conv_general_dilated | solution.py:58
  136.7 0.7 copy.57
  137.4 1.4 reshape.83
  138.8 1.1 slice.22
  139.9 6.4 %all-to-all-done.3 = f32[32,1,1152]{2,1,0:T(1,128)S(1)} async-done(((f32[32,1,1152]{2,1,0:T(1,128)}), f32[32,1,1152]{2,1,0:T(1,128)S(1)}, u32[]{:S(2)}, u32[]{:S(2)}) %all-to-all-start.3) | async-done | bytes 147488 | tf_op jit(solution)/shard_map/all_to_all | solution.py:27
  146.3 0.3 reduce.1
  146.6 0.8 reshape_reshape.3
  (11 shorter events, 0.1 us)
Async XLA Ops:
  0.6 23.5 %copy-start.1 = (bf16[32,2,8,512]{3,2,1,0:T(8,128)(2,1)S(1)}, bf16[32,2,8,512]{3,2,1,0:T(8,128)(2,1)}, u32[]{:S(2)}) copy-start(bf16[32,2,8,512]{3,2,1,0:T(8,128)(2,1)} %param.5) | copy-start | bytes 1572868
  0.6 53.5 %all-to-all-start = ((bf16[64,2,8,512]{3,2,1,0:T(8,128)(2,1)}), bf16[64,2,8,512]{3,2,1,0:T(8,128)(2,1)}, u32[]{:S(2)}, u32[]{:S(2)}) async-start(bf16[64,2,8,512]{3,2,1,0:T(8,128)(2,1)} %param.9), calls=%async_computation | async-start | bytes 2097152 | tf_op jit(solution)/shard_map/all_to_all | solution.py:94
  24.1 1.8 %copy-start.2 = (bf16[576,64]{0,1:T(8,128)(2,1)S(1)}, bf16[576,64]{0,1:T(8,128)(2,1)}, u32[]{:S(2)}) copy-start(bf16[576,64]{0,1:T(8,128)(2,1)} %param.6) | copy-start | bytes 221188
  25.9 4.1 %copy-start = (bf16[64,8,8,64]{0,3,2,1:T(8,128)(2,1)}, bf16[64,8,8,64]{0,3,2,1:T(8,128)(2,1)S(1)}, u32[]{:S(2)}) copy-start(bf16[64,8,8,64]{0,3,2,1:T(8,128)(2,1)S(1)} %copy.53) | copy-start | bytes 1572868
  34.9 0.7 copy-start.3
  35.0 0.7 copy-start.4
  126.8 19.5 %all-to-all-start.3 = ((f32[32,1,1152]{2,1,0:T(1,128)}), f32[32,1,1152]{2,1,0:T(1,128)S(1)}, u32[]{:S(2)}, u32[]{:S(2)}) async-start(f32[32,1,1152]{2,1,0:T(1,128)} %broadcast_in_dim.10), calls=%async_computation.3 | async-start | bytes 294912 | tf_op jit(solution)/shard_map/all_to_all | solution.py:27
